TPU v7x, 512 devices: a whole 4x4x16 slice. The times are simulated.
512 devices in a mesh: dp: 32 (over z, core), cent: 16 (over y, x).
Axes of the slice: x: 4, y: 4, z: 16, core: 2. Of those that a mesh axis runs over, the one named last changes fastest.
Arguments:
- points: bfloat16 [131072, 1024], P(('dp', 'cent')), may hold values from -22 to 22, as said below
- block_list: int32 [4096, 3], P(('dp', 'cent')), may hold values from 0 to 15, all different within a row; in each aligned block of 8 rows (0 to 7, 8 to 15, ...) at most 2 rows name the same one
- list_count: int32 [4096], P(('dp', 'cent')), may hold values from 1 to 3
- centroids: bfloat16 [16, 1024, 1024], P('cent', 'dp'), may hold values from -14 to 14, as said below
Outputs:
- new_centroids: float32 [16, 1024, 1024], P('cent', 'dp')
Inputs may be any that keep to these rules, and one draw needn't show every extreme that they name: `block_list`: within the rows of one device (aligned blocks of 8 rows) no block id appears more than 2 times, and the ids of one row differ. Only the first list_count[t] entries of row t of block_list are valid. `points`: Real-valued embeddings. Real-valued centroids.
All inputs are finite; a program needn't handle non-finite values.
Results may differ from a plain program's by a relative error of at most 0.0019.
Values may be sent and summed in bfloat16 or wider, within the bound.
No kernel may reach another device: no remote copies, remote signals or barrier semaphores. Data moves between devices by JAX's collectives and lax.ppermute only.
A program may use at most 64 MiB of HBM per device.

v0:
```python
import math

import jax
import jax.numpy as jnp
from jax import lax
from jax.sharding import PartitionSpec as P

score_scale = 2.0
prior_weight = 1.0


def combine_norms(peaks, totals, usable):
    keep = usable[..., None]
    highest = jnp.max(jnp.where(keep, peaks, -1e30), axis=-2)
    summed = jnp.sum(jnp.where(keep, totals * jnp.exp(peaks - highest[..., None, :]), 0.0), axis=-2)
    return highest + jnp.log(summed)


def per_device(points, block_list, list_count, centroids):
    owners = lax.axis_size("cent")
    tiles_here, listed = block_list.shape
    width = points.shape[1]
    tile_rows = points.shape[0] // tiles_here
    capacity = (tiles_here * listed + owners - 1) // owners
    slot_rows = capacity * tile_rows
    scale = score_scale / math.sqrt(width)
    usable = jnp.arange(listed, dtype=jnp.int32)[None, :] < list_count[:, None]
    naming = jnp.logical_and(
        block_list[:, :, None] == jnp.arange(owners, dtype=jnp.int32)[None, None, :],
        usable[:, :, None],
    )
    listing = jnp.any(naming, axis=1).astype(jnp.int32)
    earlier = jnp.cumsum(listing, axis=0) - listing
    placing = jnp.logical_and(
        listing.T[:, None, :] == 1,
        earlier.T[:, None, :] == jnp.arange(capacity, dtype=jnp.int32)[None, :, None],
    )
    placing = placing.astype(jnp.float32).reshape(owners * capacity, tiles_here)
    slot_rank = jnp.take_along_axis(earlier, block_list, axis=1)
    route_code = jnp.where(usable, block_list * capacity + slot_rank, -1)
    outgoing = jnp.dot(
        placing.astype(jnp.bfloat16),
        points.reshape(tiles_here, tile_rows * width),
        preferred_element_type=jnp.float32,
    )
    outgoing = outgoing.astype(jnp.bfloat16).reshape(owners, slot_rows, width)
    slot_routes = (
        jnp.dot(placing, (route_code + 1).astype(jnp.float32), precision=lax.Precision.HIGHEST)
        - 1.0
    )
    slot_routes = slot_routes.astype(jnp.bfloat16).reshape(owners, capacity, listed)
    arrived, arrived_routes = (
        lax.all_to_all(outgoing, "cent", split_axis=0, concat_axis=0, tiled=True),
        lax.all_to_all(slot_routes, "cent", split_axis=0, concat_axis=0, tiled=True),
    )
    incoming = arrived.reshape(owners * slot_rows, width)
    occupied = arrived_routes[:, :, 0] >= 0
    occupied_rows = jnp.broadcast_to(occupied[:, :, None], (owners, capacity, tile_rows)).reshape(
        -1
    )
    logits = (
        lax.dot_general(
            incoming,
            lax.all_gather(centroids, "dp", axis=1, tiled=True)[0],
            (((1,), (1,)), ((), ())),
            preferred_element_type=jnp.float32,
        )
        * scale
    )
    peaks = jnp.max(logits, axis=1)
    totals = jnp.sum(jnp.exp(logits - peaks[:, None]), axis=1)
    back_peaks, back_totals = (
        lax.all_to_all(
            peaks.reshape(owners, slot_rows), "cent", split_axis=0, concat_axis=0, tiled=True
        ),
        lax.all_to_all(
            totals.reshape(owners, slot_rows), "cent", split_axis=0, concat_axis=0, tiled=True
        ),
    )
    lookup = jnp.where(usable, route_code, 0)
    tile_norms = combine_norms(
        back_peaks.reshape(owners * capacity, tile_rows)[lookup],
        back_totals.reshape(owners * capacity, tile_rows)[lookup],
        usable,
    )
    slot_norms = jnp.dot(placing, tile_norms, precision=lax.Precision.HIGHEST)
    row_norms = lax.all_to_all(
        slot_norms.reshape(owners, slot_rows), "cent", split_axis=0, concat_axis=0, tiled=True
    ).reshape(-1)
    shares = jnp.where(occupied_rows[:, None], jnp.exp(logits - row_norms[:, None]), 0.0).astype(
        jnp.bfloat16
    )
    own_rows = centroids[0].astype(jnp.float32)
    own_count = own_rows.shape[0]
    block_mass = jnp.sum(shares, axis=0, dtype=jnp.float32)
    full_mass = lax.psum(block_mass, "dp")
    new_mass = lax.dynamic_slice_in_dim(full_mass, lax.axis_index("dp") * own_count, own_count, 0)
    block_sums = lax.dot_general(
        shares, incoming, (((0,), (0,)), ((), ())), preferred_element_type=jnp.float32
    )
    new_sums = lax.psum_scatter(block_sums, "dp", scatter_dimension=0, tiled=True)
    fresh = (new_sums + prior_weight * own_rows) / (new_mass[:, None] + prior_weight)
    return fresh[None]


def solution(mesh):
    in_specs = (
        P(("dp", "cent"), None),
        P(("dp", "cent"), None),
        P(("dp", "cent")),
        P("cent", "dp", None),
    )
    out_specs = P("cent", "dp", None)
    return jax.shard_map(
        per_device, mesh=mesh, in_specs=in_specs, out_specs=out_specs, check_vma=False
    )
```

profile of v0, /device:TPU:6, one launch (start us, length us, event | category | flops | bytes accessed | tf_op | source)
XLA Modules:
  0.0 253.5 jit_solution(3150392634497232480)
XLA Ops:
  7.3 0.7 iota_compare_fusion.1
  8.1 0.8 copy.56
  8.8 0.8 fusion.8
  10.2 0.7 gather_fusion.2
  11.4 0.7 copy.66
  12.1 9.1 %all-to-all-start = ((bf16[16,2,3]{2,1,0:T(2,128)(2,1)}), bf16[16,2,3]{2,1,0:T(2,128)(2,1)S(1)}, u32[]{:S(2)}, u32[]{:S(2)}) async-start(bf16[16,2,3]{2,1,0:T(2,128)(2,1)} %bitcast.4), calls=%async_computation | async-start | bytes 16384 | tf_op jit(solution)/shard_map/all_to_all | solution.py:54
  22.2 2.4 reshape.118
  24.6 2.2 all-to-all-done
  26.8 5.6 %all-to-all-start.1 = ((bf16[16,64,1024]{2,1,0:T(8,128)(2,1)}), bf16[16,64,1024]{2,1,0:T(8,128)(2,1)S(1)}, u32[]{:S(2)}, u32[]{:S(2)}) async-start(bf16[16,64,1024]{2,1,0:T(8,128)(2,1)} %reshape.118), calls=%async_computation.1 | async-start | bytes 4194304 | tf_op jit(solution)/shard_map/all_to_all | solution.py:53
  32.6 22.7 %all-to-all-done.1 = bf16[16,64,1024]{2,1,0:T(8,128)(2,1)S(1)} async-done(((bf16[16,64,1024]{2,1,0:T(8,128)(2,1)}), bf16[16,64,1024]{2,1,0:T(8,128)(2,1)S(1)}, u32[]{:S(2)}, u32[]{:S(2)}) %all-to-all-start.1) | async-done | bytes 2097184 | tf_op jit(solution)/shard_map/all_to_all | solution.py:53
  55.3 30.3 %all-gather.2.cloned.1.call-done = bf16[1,1024,1024]{2,1,0:T(8,128)(2,1)} async-done(((bf16[1,32,1024]{2,1,0:T(8,128)(2,1)}), bf16[1,1024,1024]{2,1,0:T(8,128)(2,1)}) %all-gather.2.cloned.1.call-update) | async-done | bytes 2097168 | tf_op jit(solution)/shard_map/all_gather | solution.py:64
  85.6 5.9 %multiply_reduce_fusion = (f32[1024]{0:T(1024)S(1)}, f32[1024,1024]{0,1:T(8,128)}) fusion(bf16[1024,1024]{1,0:T(8,128)(2,1)S(1)} %bitcast.32, bf16[1,1024,1024]{2,1,0:T(8,128)(2,1)} %all-gather.2.cloned.1.call-done), kind=kOutput, calls=%fused_computation.7 | convolution fusion | flops 2149579776 | bytes 8392704 | tf_op jit(solution)/shard_map/dot_general | solution.py:62
  92.2 7.4 %all-to-all-start.2 = ((f32[16,1,64]{2,1,0:T(1,128)}), f32[16,1,64]{2,1,0:T(1,128)S(1)}, u32[]{:S(2)}, u32[]{:S(2)}) async-start(f32[16,1,64]{2,1,0:T(1,128)} %all_to_all.26), calls=%async_computation.2 | async-start | bytes 16384 | tf_op jit(solution)/shard_map/all_to_all | solution.py:73
  99.6 2.9 %exponential_reduce_fusion = f32[1024]{0:T(1024)S(1)} fusion(f32[1024,1024]{0,1:T(8,128)} %get-tuple-element.8, f32[1024]{0:T(1024)S(1)} %get-tuple-element.7), kind=kLoop, calls=%fused_computation.6 | loop fusion | flops 3144704 | bytes 4202496 | tf_op jit(solution)/shard_map/reduce_sum | solution.py:71
  103.2 1.9 all-to-all-done.2
  105.1 5.3 %all-to-all-start.3 = ((f32[16,1,64]{2,1,0:T(1,128)}), f32[16,1,64]{2,1,0:T(1,128)S(1)}, u32[]{:S(2)}, u32[]{:S(2)}) async-start(f32[16,1,64]{2,1,0:T(1,128)} %all_to_all.28), calls=%async_computation.3 | async-start | bytes 16384 | tf_op jit(solution)/shard_map/all_to_all | solution.py:76
  112.3 3.7 %all-to-all-done.3 = f32[16,1,64]{2,1,0:T(1,128)S(1)} async-done(((f32[16,1,64]{2,1,0:T(1,128)}), f32[16,1,64]{2,1,0:T(1,128)S(1)}, u32[]{:S(2)}, u32[]{:S(2)}) %all-to-all-start.3) | async-done | bytes 4128 | tf_op jit(solution)/shard_map/all_to_all | solution.py:76
  118.2 5.3 %all-to-all-start.4 = ((f32[16,1,64]{2,1,0:T(1,128)}), f32[16,1,64]{2,1,0:T(1,128)S(1)}, u32[]{:S(2)}, u32[]{:S(2)}) async-start(f32[16,1,64]{2,1,0:T(1,128)} %bitcast.9), calls=%async_computation.4 | async-start | bytes 16384 | tf_op jit(solution)/shard_map/all_to_all | solution.py:87
  123.9 5.2 %all-to-all-done.4 = f32[16,1,64]{2,1,0:T(1,128)S(1)} async-done(((f32[16,1,64]{2,1,0:T(1,128)}), f32[16,1,64]{2,1,0:T(1,128)S(1)}, u32[]{:S(2)}, u32[]{:S(2)}) %all-to-all-start.4) | async-done | bytes 4128 | tf_op jit(solution)/shard_map/all_to_all | solution.py:87
  129.8 6.5 %fusion.5 = f32[1024,1024]{1,0:T(8,128)} fusion(bf16[1024,1024]{1,0:T(8,128)(2,1)S(1)} %bitcast.33, f32[1024,1024]{0,1:T(8,128)} %get-tuple-element.8, f32[1024]{0:T(1024)S(1)} %sub.44, pred[1024]{0:T(1024)(128)(4,1)S(1)} %broadcast_in_dim.67), kind=kOutput, calls=%fused_computation.15 | convolution fusion | flops 2151677952 | bytes 10490880 | tf_op jit(solution)/shard_map/dot_general | solution.py:98
  136.3 3.1 %convert_reduce_fusion = f32[1024]{0:T(1024)S(1)} fusion(f32[1024]{0:T(1024)S(1)} %sub.44, f32[1024,1024]{0,1:T(8,128)} %get-tuple-element.8, pred[1024]{0:T(1024)(128)(4,1)S(1)} %broadcast_in_dim.67), kind=kLoop, calls=%fused_computation.4 | loop fusion | flops 6290432 | bytes 4203520 | tf_op jit(solution)/shard_map/reduce_sum | solution.py:95
  139.4 45.8 %psum.7 = f32[1024]{0:T(1024)S(1)} all-reduce(f32[1024]{0:T(1024)S(1)} %convert_reduce_fusion), channel_id=1, replica_groups=mesh['dp'=32,'cent'=16] {'dp'}, use_global_device_ids=true, to_apply=%region_8.9 | all-reduce | flops 1024 | bytes 8192 | tf_op jit(solution)/shard_map/psum | solution.py:96
  185.3 59.7 %reduce-scatter.2.cloned.1.call-done = f32[32,1024]{1,0:T(8,128)} async-done(((f32[1024,1024]{1,0:T(8,128)}), f32[32,1024]{1,0:T(8,128)}) %reduce-scatter.2.cloned.1.call-update) | async-done | bytes 131088 | tf_op jit(solution)/shard_map/reduce_scatter | solution.py:101
  245.0 1.6 fusion.4
  (58 shorter events, 9.6 us)
Async XLA Ops:
  6.5 4.6 %copy-start.2 = (s32[8]{0:T(128)S(1)}, s32[8]{0:T(128)}, u32[]{:S(2)}) copy-start(s32[8]{0:T(128)} %param.6) | copy-start | bytes 100
  6.5 14.7 %copy-start = (bf16[256,1024]{1,0:T(8,128)(2,1)S(1)}, bf16[256,1024]{1,0:T(8,128)(2,1)}, u32[]{:S(2)}) copy-start(bf16[256,1024]{1,0:T(8,128)(2,1)} %param.4) | copy-start | bytes 1572868
  6.5 79.1 %all-gather.2.cloned.1.call-start = ((), (), s32[]{:S(2)}) async-start(), calls=%async_computation.6 | async-start | bytes 2162688 | tf_op jit(solution)/shard_map/all_gather | solution.py:64
  12.1 14.7 %all-to-all-start = ((bf16[16,2,3]{2,1,0:T(2,128)(2,1)}), bf16[16,2,3]{2,1,0:T(2,128)(2,1)S(1)}, u32[]{:S(2)}, u32[]{:S(2)}) async-start(bf16[16,2,3]{2,1,0:T(2,128)(2,1)} %bitcast.4), calls=%async_computation | async-start | bytes 16384 | tf_op jit(solution)/shard_map/all_to_all | solution.py:54
  26.8 28.5 %all-to-all-start.1 = ((bf16[16,64,1024]{2,1,0:T(8,128)(2,1)}), bf16[16,64,1024]{2,1,0:T(8,128)(2,1)S(1)}, u32[]{:S(2)}, u32[]{:S(2)}) async-start(bf16[16,64,1024]{2,1,0:T(8,128)(2,1)} %reshape.118), calls=%async_computation.1 | async-start | bytes 4194304 | tf_op jit(solution)/shard_map/all_to_all | solution.py:53
  92.2 12.9 %all-to-all-start.2 = ((f32[16,1,64]{2,1,0:T(1,128)}), f32[16,1,64]{2,1,0:T(1,128)S(1)}, u32[]{:S(2)}, u32[]{:S(2)}) async-start(f32[16,1,64]{2,1,0:T(1,128)} %all_to_all.26), calls=%async_computation.2 | async-start | bytes 16384 | tf_op jit(solution)/shard_map/all_to_all | solution.py:73
  105.1 10.9 %all-to-all-start.3 = ((f32[16,1,64]{2,1,0:T(1,128)}), f32[16,1,64]{2,1,0:T(1,128)S(1)}, u32[]{:S(2)}, u32[]{:S(2)}) async-start(f32[16,1,64]{2,1,0:T(1,128)} %all_to_all.28), calls=%async_computation.3 | async-start | bytes 16384 | tf_op jit(solution)/shard_map/all_to_all | solution.py:76
  118.2 10.9 %all-to-all-start.4 = ((f32[16,1,64]{2,1,0:T(1,128)}), f32[16,1,64]{2,1,0:T(1,128)S(1)}, u32[]{:S(2)}, u32[]{:S(2)}) async-start(f32[16,1,64]{2,1,0:T(1,128)} %bitcast.9), calls=%async_computation.4 | async-start | bytes 16384 | tf_op jit(solution)/shard_map/all_to_all | solution.py:87
  123.5 121.5 %reduce-scatter.2.cloned.1.call-start = ((), (), s32[]{:S(2)}) async-start(), calls=%async_computation.7 | async-start | bytes 4325376 | tf_op jit(solution)/shard_map/reduce_scatter | solution.py:101
  136.3 108.7 %copy-start.1 = (bf16[1,32,1024]{2,1,0:T(8,128)(2,1)S(1)}, bf16[1,32,1024]{2,1,0:T(8,128)(2,1)}, u32[]{:S(2)}) copy-start(bf16[1,32,1024]{2,1,0:T(8,128)(2,1)} %param.7) | copy-start | bytes 196612
Sparse Core Ops, SparseCore 0:
  9.5 76.1 all-gather.1
  136.4 108.5 reduce-scatter.1
where the time goes:
time: 254 us; the launch traced here: 253 us
  waiting for transfers between devices  126 us (50%)
  blocking collectives  45.8 us (18%)
  starting transfers between devices  32.8 us (13%)
  between operations  13.5 us (5%)
  matrix products  13.4 us (5%)
  other arithmetic  11.5 us (5%)
  local copies, waits for them, and re-layouts  9.97 us (4%)
    reduce_scatter x1, waiting for transfers between devices, per_device(): lax.psum_scatter(block_sums, 'dp', scatter_dimension=0, tiled=True)  59.7 us
    psum x1, blocking collectives, per_device(): full_mass = lax.psum(block_mass, 'dp')  45.8 us
    all_gather x1, waiting for transfers between devices, per_device(): lax.all_gather(centroids, 'dp', axis=1, tiled=True)[0]  30.3 us
    all_to_all x1, waiting for transfers between devices, per_device(): lax.all_to_all(outgoing, 'cent', split_axis=0, concat_axis=0, tiled=True)  22.7 us
    all_to_all x1, starting transfers between devices, per_device(): lax.all_to_all(slot_routes, 'cent', split_axis=0, concat_axis=0, tiled=True)  9.12 us
    all_to_all x1, starting transfers between devices, per_device(): lax.all_to_all(peaks.reshape(owners, slot_rows), 'cent', split_axis=0, co...  7.35 us
    dot_general x1, matrix products, per_device(): lax.dot_general(shares, incoming, (((0,), (0,)), ((), ())), preferred_ele...  6.49 us
    dot_general x1, matrix products, per_device(): lax.dot_general(incoming, lax.all_gather(centroids, 'dp', axis=1, tiled=T...  5.88 us
  transfers between devices with their start and end apart: 7, of which 7 were waited for; matrix products, arithmetic and copies ran while one was open for 7% of the time, Pallas kernels for 0%

commit v1 on v0

--- a/solution.py
+++ b/solution.py
@@ -7,6 +7,7 @@
 
 score_scale = 2.0
 prior_weight = 1.0
+empty_norm = 1e30
 
 
 def combine_norms(peaks, totals, usable):
@@ -44,20 +45,8 @@
         preferred_element_type=jnp.float32,
     )
     outgoing = outgoing.astype(jnp.bfloat16).reshape(owners, slot_rows, width)
-    slot_routes = (
-        jnp.dot(placing, (route_code + 1).astype(jnp.float32), precision=lax.Precision.HIGHEST)
-        - 1.0
-    )
-    slot_routes = slot_routes.astype(jnp.bfloat16).reshape(owners, capacity, listed)
-    arrived, arrived_routes = (
-        lax.all_to_all(outgoing, "cent", split_axis=0, concat_axis=0, tiled=True),
-        lax.all_to_all(slot_routes, "cent", split_axis=0, concat_axis=0, tiled=True),
-    )
+    arrived = lax.all_to_all(outgoing, "cent", split_axis=0, concat_axis=0, tiled=True)
     incoming = arrived.reshape(owners * slot_rows, width)
-    occupied = arrived_routes[:, :, 0] >= 0
-    occupied_rows = jnp.broadcast_to(occupied[:, :, None], (owners, capacity, tile_rows)).reshape(
-        -1
-    )
     logits = (
         lax.dot_general(
             incoming,
@@ -69,36 +58,34 @@
     )
     peaks = jnp.max(logits, axis=1)
     totals = jnp.sum(jnp.exp(logits - peaks[:, None]), axis=1)
-    back_peaks, back_totals = (
-        lax.all_to_all(
-            peaks.reshape(owners, slot_rows), "cent", split_axis=0, concat_axis=0, tiled=True
-        ),
-        lax.all_to_all(
-            totals.reshape(owners, slot_rows), "cent", split_axis=0, concat_axis=0, tiled=True
-        ),
+    stats = jnp.stack(
+        [peaks.reshape(owners, slot_rows), totals.reshape(owners, slot_rows)], axis=1
     )
+    back = lax.all_to_all(stats, "cent", split_axis=0, concat_axis=0, tiled=True)
+    back_peaks = back[:, 0].reshape(owners * capacity, tile_rows)
+    back_totals = back[:, 1].reshape(owners * capacity, tile_rows)
     lookup = jnp.where(usable, route_code, 0)
-    tile_norms = combine_norms(
-        back_peaks.reshape(owners * capacity, tile_rows)[lookup],
-        back_totals.reshape(owners * capacity, tile_rows)[lookup],
-        usable,
+    tile_norms = combine_norms(back_peaks[lookup], back_totals[lookup], usable)
+    empty = 1.0 - jnp.sum(placing, axis=1)
+    slot_norms = (
+        jnp.dot(placing, tile_norms, precision=lax.Precision.HIGHEST)
+        + empty[:, None] * empty_norm
     )
-    slot_norms = jnp.dot(placing, tile_norms, precision=lax.Precision.HIGHEST)
     row_norms = lax.all_to_all(
         slot_norms.reshape(owners, slot_rows), "cent", split_axis=0, concat_axis=0, tiled=True
     ).reshape(-1)
-    shares = jnp.where(occupied_rows[:, None], jnp.exp(logits - row_norms[:, None]), 0.0).astype(
-        jnp.bfloat16
+    shares = jnp.exp(logits - row_norms[:, None]).astype(jnp.bfloat16)
+    own_rows = centroids[0].astype(jnp.float32)
+    marker = (jnp.arange(128, dtype=jnp.int32) == 0).astype(jnp.bfloat16)
+    widened = jnp.concatenate(
+        [incoming, jnp.broadcast_to(marker[None, :], (incoming.shape[0], 128))], axis=1
     )
-    own_rows = centroids[0].astype(jnp.float32)
-    own_count = own_rows.shape[0]
-    block_mass = jnp.sum(shares, axis=0, dtype=jnp.float32)
-    full_mass = lax.psum(block_mass, "dp")
-    new_mass = lax.dynamic_slice_in_dim(full_mass, lax.axis_index("dp") * own_count, own_count, 0)
     block_sums = lax.dot_general(
-        shares, incoming, (((0,), (0,)), ((), ())), preferred_element_type=jnp.float32
+        shares, widened, (((0,), (0,)), ((), ())), preferred_element_type=jnp.float32
     )
-    new_sums = lax.psum_scatter(block_sums, "dp", scatter_dimension=0, tiled=True)
+    reduced = lax.psum_scatter(block_sums, "dp", scatter_dimension=0, tiled=True)
+    new_sums = reduced[:, :width]
+    new_mass = reduced[:, width]
     fresh = (new_sums + prior_weight * own_rows) / (new_mass[:, None] + prior_weight)
     return fresh[None]
 

time: 254 us -> 251 us (0.988)
  waiting for transfers between devices: 126 us -> 182 us
  blocking collectives: 45.8 us -> 0 us
  starting transfers between devices: 32.8 us -> 22.1 us
  other arithmetic: 11.5 us -> 8.68 us
    reduce_scatter x1, waiting for transfers between devices: 59.7 us -> 110 us  [per_device(): lax.psum_scatter(block_sums, 'dp', scatter_dimension=0, tiled=True)]
    psum x1 -> x0, blocking collectives: 45.8 us -> none  [per_device(): full_mass = lax.psum(block_mass, 'dp')]
    all_to_all x3 -> x1, starting transfers between devices: 21.8 us -> 7.25 us  [per_device(): lax.all_to_all(stats, 'cent', split_axis=0, concat_axis=0, tiled=True)]
    all_gather x1, waiting for transfers between devices: 30.3 us -> 38.8 us  [per_device(): lax.all_gather(centroids, 'dp', axis=1, tiled=True)[0]]
    all_to_all x1, starting transfers between devices: 5.59 us -> 9.5 us  [per_device(): lax.all_to_all(outgoing, 'cent', split_axis=0, concat_axis=0, tiled=True)]
    reduce_sum x1, other arithmetic: 3.08 us -> 0.1 us  [per_device(): empty = 1.0 - jnp.sum(placing, axis=1)]
    all_to_all x3 -> x1, waiting for transfers between devices: 7.81 us -> 5.28 us  [per_device(): lax.all_to_all(stats, 'cent', split_axis=0, concat_axis=0, tiled=True)]
    dot_general x3 -> x2, matrix products: 6.87 us -> 7.58 us  [the longest x1 7.39 us: per_device(): lax.dot_general(shares, widened, (((0,), (0,)), ((), ())), preferred_elem...]
  transfers between devices with their start and end apart: 7 -> 5, of which waited for: 7 -> 5; matrix products, arithmetic and copies ran while one was open for 7% -> 3% of each run, Pallas kernels for 0% -> 0%
where the time goes in v1:
time: 251 us; the launch traced here: 250 us
  waiting for transfers between devices  182 us (73%)
  starting transfers between devices  22.1 us (9%)
  matrix products  14.2 us (6%)
  between operations  13.6 us (5%)
  local copies, waits for them, and re-layouts  9.44 us (4%)
  other arithmetic  8.68 us (3%)
    reduce_scatter x1, waiting for transfers between devices, per_device(): lax.psum_scatter(block_sums, 'dp', scatter_dimension=0, tiled=True)  110 us
    all_gather x1, waiting for transfers between devices, per_device(): lax.all_gather(centroids, 'dp', axis=1, tiled=True)[0]  38.8 us
    all_to_all x1, waiting for transfers between devices, per_device(): lax.all_to_all(outgoing, 'cent', split_axis=0, concat_axis=0, tiled=True)  22.5 us
    all_to_all x1, starting transfers between devices, per_device(): lax.all_to_all(outgoing, 'cent', split_axis=0, concat_axis=0, tiled=True)  9.5 us
    dot_general x1, matrix products, per_device(): lax.dot_general(shares, widened, (((0,), (0,)), ((), ())), preferred_elem...  7.39 us
    all_to_all x1, starting transfers between devices, per_device(): lax.all_to_all(stats, 'cent', split_axis=0, concat_axis=0, tiled=True)  7.25 us
    dot_general x1, matrix products, per_device(): lax.dot_general(incoming, lax.all_gather(centroids, 'dp', axis=1, tiled=T...  5.99 us
    all_to_all x1, waiting for transfers between devices, per_device(): lax.all_to_all(slot_norms.reshape(owners, slot_rows), 'cent', split_axis=...  5.48 us
  transfers between devices with their start and end apart: 5, of which 5 were waited for; matrix products, arithmetic and copies ran while one was open for 3% of the time, Pallas kernels for 0%

profile of v1, /device:TPU:6, one launch (start us, length us, event | category | flops | bytes accessed | tf_op | source)
XLA Modules:
  0.0 250.4 jit_solution(18403319197507277494)
XLA Ops:
  6.5 0.7 all-gather.2.cloned.1.call-update
  7.3 0.7 iota_compare_fusion.1
  8.1 0.8 fusion.16
  9.1 1.3 reshape.116
  10.4 0.7 convolution_convert_fusion
  11.1 2.4 reshape.117
  13.4 9.5 %all-to-all-start = ((bf16[16,64,1024]{2,1,0:T(8,128)(2,1)}), bf16[16,64,1024]{2,1,0:T(8,128)(2,1)S(1)}, u32[]{:S(2)}, u32[]{:S(2)}) async-start(bf16[16,64,1024]{2,1,0:T(8,128)(2,1)} %reshape.117), calls=%async_computation | async-start | bytes 4194304 | tf_op jit(solution)/shard_map/all_to_all | solution.py:48
  23.3 0.7 gather_fusion.2
  24.4 22.5 %all-to-all-done = bf16[16,64,1024]{2,1,0:T(8,128)(2,1)S(1)} async-done(((bf16[16,64,1024]{2,1,0:T(8,128)(2,1)}), bf16[16,64,1024]{2,1,0:T(8,128)(2,1)S(1)}, u32[]{:S(2)}, u32[]{:S(2)}) %all-to-all-start) | async-done | bytes 2097184 | tf_op jit(solution)/shard_map/all_to_all | solution.py:48
  46.9 38.8 %all-gather.2.cloned.1.call-done = bf16[1,1024,1024]{2,1,0:T(8,128)(2,1)} async-done(((bf16[1,32,1024]{2,1,0:T(8,128)(2,1)}), bf16[1,1024,1024]{2,1,0:T(8,128)(2,1)}) %all-gather.2.cloned.1.call-update) | async-done | bytes 2097168 | tf_op jit(solution)/shard_map/all_gather | solution.py:53
  85.7 6.0 %multiply_reduce_fusion = (f32[1024]{0:T(1024)S(1)}, f32[1024,1024]{0,1:T(8,128)}) fusion(bf16[1024,1024]{1,0:T(8,128)(2,1)S(1)} %bitcast.25, bf16[1,1024,1024]{2,1,0:T(8,128)(2,1)} %all-gather.2.cloned.1.call-done), kind=kOutput, calls=%fused_computation.6 | convolution fusion | flops 2149579776 | bytes 8392704 | tf_op jit(solution)/shard_map/dot_general | solution.py:51
  91.8 2.9 %exponential_reduce_fusion = f32[1024]{0:T(1024)S(1)} fusion(f32[1024,1024]{0,1:T(8,128)} %get-tuple-element.10, f32[1024]{0:T(1024)S(1)} %get-tuple-element.9), kind=kLoop, calls=%fused_computation.5 | loop fusion | flops 3144704 | bytes 4202496 | tf_op jit(solution)/shard_map/reduce_sum | solution.py:60
  94.8 0.7 reshape.173
  95.5 7.3 %all-to-all-start.1 = ((f32[16,1,128]{2,1,0:T(1,128)}), f32[16,1,128]{2,1,0:T(1,128)S(1)}, u32[]{:S(2)}, u32[]{:S(2)}) async-start(f32[16,1,128]{2,1,0:T(1,128)} %reshape.173), calls=%async_computation.1 | async-start | bytes 16384 | tf_op jit(solution)/shard_map/all_to_all | solution.py:64
  103.0 5.3 %all-to-all-done.1 = f32[16,1,128]{2,1,0:T(1,128)S(1)} async-done(((f32[16,1,128]{2,1,0:T(1,128)}), f32[16,1,128]{2,1,0:T(1,128)S(1)}, u32[]{:S(2)}, u32[]{:S(2)}) %all-to-all-start.1) | async-done | bytes 8224 | tf_op jit(solution)/shard_map/all_to_all | solution.py:64
  108.8 0.7 reduce.15
  111.3 0.7 all_to_all.14
  112.0 5.3 %all-to-all-start.2 = ((f32[16,1,64]{2,1,0:T(1,128)}), f32[16,1,64]{2,1,0:T(1,128)S(1)}, u32[]{:S(2)}, u32[]{:S(2)}) async-start(f32[16,1,64]{2,1,0:T(1,128)} %bitcast.7), calls=%async_computation.2 | async-start | bytes 16384 | tf_op jit(solution)/shard_map/all_to_all | solution.py:74
  117.4 5.5 %all-to-all-done.2 = f32[16,1,64]{2,1,0:T(1,128)S(1)} async-done(((f32[16,1,64]{2,1,0:T(1,128)}), f32[16,1,64]{2,1,0:T(1,128)S(1)}, u32[]{:S(2)}, u32[]{:S(2)}) %all-to-all-start.2) | async-done | bytes 4128 | tf_op jit(solution)/shard_map/all_to_all | solution.py:74
  123.4 0.7 reduce.14
  124.1 7.4 %fusion = f32[1024,1152]{1,0:T(8,128)} fusion(bf16[1024,1024]{1,0:T(8,128)(2,1)S(1)} %bitcast.26, f32[1024,1024]{0,1:T(8,128)} %get-tuple-element.10, f32[1024]{0:T(1024)S(1)} %sub.54, bf16[1152]{0:T(1024)(128)(2,1)S(1)} %pad.1.clone), kind=kOutput, calls=%fused_computation.7 | convolution fusion | flops 2423783424 | bytes 11016448 | tf_op jit(solution)/shard_map/dot_general | solution.py:83
  131.5 109.6 %reduce-scatter.2.cloned.1.call-done = f32[32,1152]{1,0:T(8,128)} async-done(((f32[1024,1152]{1,0:T(8,128)}), f32[32,1152]{1,0:T(8,128)}) %reduce-scatter.2.cloned.1.call-update) | async-done | bytes 147472 | tf_op jit(solution)/shard_map/reduce_scatter | solution.py:86
  241.1 0.8 fusion.10
  241.9 1.6 fusion.9
  (53 shorter events, 4.4 us)
Async XLA Ops:
  6.5 79.2 %all-gather.2.cloned.1.call-start = ((), (), s32[]{:S(2)}) async-start(), calls=%async_computation.4 | async-start | bytes 2162688 | tf_op jit(solution)/shard_map/all_gather | solution.py:53
  11.0 11.9 %copy-start.1 = (s32[8,3]{0,1:T(4,128)S(1)}, s32[8,3]{0,1:T(4,128)}, u32[]{:S(2)}) copy-start(s32[8,3]{0,1:T(4,128)} %param.5) | copy-start | bytes 292
  13.4 10.7 %copy-start.2 = (s32[8]{0:T(128)S(1)}, s32[8]{0:T(128)}, u32[]{:S(2)}) copy-start(s32[8]{0:T(128)} %param.6) | copy-start | bytes 100
  13.4 33.4 %all-to-all-start = ((bf16[16,64,1024]{2,1,0:T(8,128)(2,1)}), bf16[16,64,1024]{2,1,0:T(8,128)(2,1)S(1)}, u32[]{:S(2)}, u32[]{:S(2)}) async-start(bf16[16,64,1024]{2,1,0:T(8,128)(2,1)} %reshape.117), calls=%async_computation | async-start | bytes 4194304 | tf_op jit(solution)/shard_map/all_to_all | solution.py:48
  95.5 12.8 %all-to-all-start.1 = ((f32[16,1,128]{2,1,0:T(1,128)}), f32[16,1,128]{2,1,0:T(1,128)S(1)}, u32[]{:S(2)}, u32[]{:S(2)}) async-start(f32[16,1,128]{2,1,0:T(1,128)} %reshape.173), calls=%async_computation.1 | async-start | bytes 16384 | tf_op jit(solution)/shard_map/all_to_all | solution.py:64
  112.0 10.9 %all-to-all-start.2 = ((f32[16,1,64]{2,1,0:T(1,128)}), f32[16,1,64]{2,1,0:T(1,128)S(1)}, u32[]{:S(2)}, u32[]{:S(2)}) async-start(f32[16,1,64]{2,1,0:T(1,128)} %bitcast.7), calls=%async_computation.2 | async-start | bytes 16384 | tf_op jit(solution)/shard_map/all_to_all | solution.py:74
  117.3 123.8 %reduce-scatter.2.cloned.1.call-start = ((), (), s32[]{:S(2)}) async-start(), calls=%async_computation.5 | async-start | bytes 4866048 | tf_op jit(solution)/shard_map/reduce_scatter | solution.py:86
  131.5 110.4 %copy-start = (bf16[1,32,1024]{2,1,0:T(8,128)(2,1)S(1)}, bf16[1,32,1024]{2,1,0:T(8,128)(2,1)}, u32[]{:S(2)}) copy-start(bf16[1,32,1024]{2,1,0:T(8,128)(2,1)} %param.7) | copy-start | bytes 196612
Sparse Core Ops, SparseCore 0:
  9.5 76.1 all-gather.1
  131.6 109.3 reduce-scatter.1

commit v2 on v1

--- a/solution.py
+++ b/solution.py
@@ -3,7 +3,7 @@
 import jax
 import jax.numpy as jnp
 from jax import lax
-from jax.sharding import PartitionSpec as P
+from jax.sharding import Mesh, PartitionSpec as P
 
 score_scale = 2.0
 prior_weight = 1.0
@@ -50,7 +50,7 @@
     logits = (
         lax.dot_general(
             incoming,
-            lax.all_gather(centroids, "dp", axis=1, tiled=True)[0],
+            lax.all_gather(centroids, ("z", "core"), axis=1, tiled=True)[0],
             (((1,), (1,)), ((), ())),
             preferred_element_type=jnp.float32,
         )
@@ -83,7 +83,13 @@
     block_sums = lax.dot_general(
         shares, widened, (((0,), (0,)), ((), ())), preferred_element_type=jnp.float32
     )
-    reduced = lax.psum_scatter(block_sums, "dp", scatter_dimension=0, tiled=True)
+    n_core = lax.axis_size("core")
+    core = lax.axis_index("core")
+    by_owner = block_sums.reshape(lax.axis_size("z"), n_core, -1, block_sums.shape[1])
+    mine = lax.dynamic_index_in_dim(by_owner, core, axis=1, keepdims=False)
+    other = lax.dynamic_index_in_dim(by_owner, n_core - 1 - core, axis=1, keepdims=False)
+    paired = mine + lax.ppermute(other, "core", [(0, 1), (1, 0)])
+    reduced = lax.psum_scatter(paired, "z", scatter_dimension=0, tiled=True)[0]
     new_sums = reduced[:, :width]
     new_mass = reduced[:, width]
     fresh = (new_sums + prior_weight * own_rows) / (new_mass[:, None] + prior_weight)
@@ -91,13 +97,19 @@
 
 
 def solution(mesh):
+    cores = 2
+    split = Mesh(
+        mesh.devices.reshape(mesh.shape["dp"] // cores, cores, mesh.shape["cent"]),
+        ("z", "core", "cent"),
+    )
+    rows = ("z", "core")
     in_specs = (
-        P(("dp", "cent"), None),
-        P(("dp", "cent"), None),
-        P(("dp", "cent")),
-        P("cent", "dp", None),
+        P((*rows, "cent"), None),
+        P((*rows, "cent"), None),
+        P((*rows, "cent")),
+        P("cent", rows, None),
     )
-    out_specs = P("cent", "dp", None)
+    out_specs = P("cent", rows, None)
     return jax.shard_map(
-        per_device, mesh=mesh, in_specs=in_specs, out_specs=out_specs, check_vma=False
+        per_device, mesh=split, in_specs=in_specs, out_specs=out_specs, check_vma=False
     )

time: 251 us -> 221 us (0.88)
  waiting for transfers between devices: 182 us -> 146 us
  other arithmetic: 8.68 us -> 12 us
  local copies, waits for them, and re-layouts: 9.44 us -> 12.2 us
    reduce_scatter x1, waiting for transfers between devices: 110 us -> 68.8 us  [per_device(): reduced = lax.psum_scatter(paired, 'z', scatter_dimension=0, tiled=True)[0]]
    ppermute x0 -> x1, waiting for transfers between devices: none -> 4.71 us  [per_device(): paired = mine + lax.ppermute(other, 'core', [(0, 1), (1, 0)])]
    add x0 -> x1, other arithmetic: none -> 3.36 us  [per_device(): paired = mine + lax.ppermute(other, 'core', [(0, 1), (1, 0)])]
  transfers between devices with their start and end apart: 5 -> 6, of which waited for: 5 -> 6; matrix products, arithmetic and copies ran while one was open for 3% -> 4% of each run, Pallas kernels for 0% -> 0%
where the time goes in v2:
time: 221 us; the launch traced here: 220 us
  waiting for transfers between devices  146 us (66%)
  starting transfers between devices  24 us (11%)
  between operations  13.6 us (6%)
  local copies, waits for them, and re-layouts  12.2 us (6%)
  other arithmetic  12 us (5%)
  matrix products  11.7 us (5%)
    reduce_scatter x1, waiting for transfers between devices, per_device(): reduced = lax.psum_scatter(paired, 'z', scatter_dimension=0, tiled=True)[0]  68.8 us
    all_gather x1, waiting for transfers between devices, per_device(): lax.all_gather(centroids, ('z', 'core'), axis=1, tiled=True)[0]  38.8 us
    all_to_all x1, waiting for transfers between devices, per_device(): lax.all_to_all(outgoing, 'cent', split_axis=0, concat_axis=0, tiled=True)  22.5 us
    all_to_all x1, starting transfers between devices, per_device(): lax.all_to_all(outgoing, 'cent', split_axis=0, concat_axis=0, tiled=True)  9.5 us
    all_to_all x1, starting transfers between devices, per_device(): lax.all_to_all(stats, 'cent', split_axis=0, concat_axis=0, tiled=True)  7.26 us
    dot_general x1, matrix products, per_device(): lax.dot_general(incoming, lax.all_gather(centroids, ('z', 'core'), axis=1...  5.89 us
    all_to_all x1, waiting for transfers between devices, per_device(): lax.all_to_all(slot_norms.reshape(owners, slot_rows), 'cent', split_axis=...  5.48 us
    all_to_all x1, starting transfers between devices, per_device(): lax.all_to_all(slot_norms.reshape(owners, slot_rows), 'cent', split_axis=...  5.34 us
  transfers between devices with their start and end apart: 6, of which 6 were waited for; matrix products, arithmetic and copies ran while one was open for 4% of the time, Pallas kernels for 0%

profile of v2, /device:TPU:6, one launch (start us, length us, event | category | flops | bytes accessed | tf_op | source)
XLA Modules:
  0.0 220.0 jit_solution(7488559341657853877)
XLA Ops:
  6.5 0.7 all-gather.2.cloned.1.call-update
  7.3 0.7 iota_compare_fusion.1
  8.1 0.8 fusion.16
  9.1 1.3 reshape.119
  11.0 2.4 %reshape.120 = bf16[16,64,1024]{2,1,0:T(8,128)(2,1)} reshape(bf16[32,32768]{1,0:T(8,128)(2,1)S(1)} %convolution_convert_fusion) | data formatting | bytes 4194304 | tf_op jit(solution)/shard_map/reshape | solution.py:47
  13.4 9.5 %all-to-all-start = ((bf16[16,64,1024]{2,1,0:T(8,128)(2,1)}), bf16[16,64,1024]{2,1,0:T(8,128)(2,1)S(1)}, u32[]{:S(2)}, u32[]{:S(2)}) async-start(bf16[16,64,1024]{2,1,0:T(8,128)(2,1)} %reshape.120), calls=%async_computation | async-start | bytes 4194304 | tf_op jit(solution)/shard_map/all_to_all | solution.py:48
  23.3 0.7 gather_fusion.2
  24.4 22.5 %all-to-all-done = bf16[16,64,1024]{2,1,0:T(8,128)(2,1)S(1)} async-done(((bf16[16,64,1024]{2,1,0:T(8,128)(2,1)}), bf16[16,64,1024]{2,1,0:T(8,128)(2,1)S(1)}, u32[]{:S(2)}, u32[]{:S(2)}) %all-to-all-start) | async-done | bytes 2097184 | tf_op jit(solution)/shard_map/all_to_all | solution.py:48
  46.9 38.8 %all-gather.2.cloned.1.call-done = bf16[1,1024,1024]{2,1,0:T(8,128)(2,1)} async-done(((bf16[1,32,1024]{2,1,0:T(8,128)(2,1)}), bf16[1,1024,1024]{2,1,0:T(8,128)(2,1)}) %all-gather.2.cloned.1.call-update) | async-done | bytes 2097168 | tf_op jit(solution)/shard_map/all_gather | solution.py:53
  85.7 5.9 %multiply_reduce_fusion = (f32[1024]{0:T(1024)S(1)}, f32[1024,1024]{0,1:T(8,128)}) fusion(bf16[1024,1024]{1,0:T(8,128)(2,1)S(1)} %bitcast.33, bf16[1,1024,1024]{2,1,0:T(8,128)(2,1)} %all-gather.2.cloned.1.call-done), kind=kOutput, calls=%fused_computation.6 | convolution fusion | flops 2149579776 | bytes 8392704 | tf_op jit(solution)/shard_map/dot_general | solution.py:51
  91.7 2.9 %exponential_reduce_fusion = f32[1024]{0:T(1024)S(1)} fusion(f32[1024,1024]{0,1:T(8,128)} %get-tuple-element.10, f32[1024]{0:T(1024)S(1)} %get-tuple-element.9), kind=kLoop, calls=%fused_computation.5 | loop fusion | flops 3144704 | bytes 4202496 | tf_op jit(solution)/shard_map/reduce_sum | solution.py:60
  95.4 7.3 %all-to-all-start.1 = ((f32[16,1,128]{2,1,0:T(1,128)}), f32[16,1,128]{2,1,0:T(1,128)S(1)}, u32[]{:S(2)}, u32[]{:S(2)}) async-start(f32[16,1,128]{2,1,0:T(1,128)} %reshape.177), calls=%async_computation.1 | async-start | bytes 16384 | tf_op jit(solution)/shard_map/all_to_all | solution.py:64
  102.9 5.3 %all-to-all-done.1 = f32[16,1,128]{2,1,0:T(1,128)S(1)} async-done(((f32[16,1,128]{2,1,0:T(1,128)}), f32[16,1,128]{2,1,0:T(1,128)S(1)}, u32[]{:S(2)}, u32[]{:S(2)}) %all-to-all-start.1) | async-done | bytes 8224 | tf_op jit(solution)/shard_map/all_to_all | solution.py:64
  111.9 5.3 %all-to-all-start.2 = ((f32[16,1,64]{2,1,0:T(1,128)}), f32[16,1,64]{2,1,0:T(1,128)S(1)}, u32[]{:S(2)}, u32[]{:S(2)}) async-start(f32[16,1,64]{2,1,0:T(1,128)} %bitcast.7), calls=%async_computation.2 | async-start | bytes 16384 | tf_op jit(solution)/shard_map/all_to_all | solution.py:74
  117.3 5.5 %all-to-all-done.2 = f32[16,1,64]{2,1,0:T(1,128)S(1)} async-done(((f32[16,1,64]{2,1,0:T(1,128)}), f32[16,1,64]{2,1,0:T(1,128)S(1)}, u32[]{:S(2)}, u32[]{:S(2)}) %all-to-all-start.2) | async-done | bytes 4128 | tf_op jit(solution)/shard_map/all_to_all | solution.py:74
  124.0 5.0 %fusion = f32[1024,1152]{1,0:T(8,128)S(1)} fusion(bf16[1024,1024]{1,0:T(8,128)(2,1)S(1)} %bitcast.34, f32[1024,1024]{0,1:T(8,128)} %get-tuple-element.10, f32[1024]{0:T(1024)S(1)} %sub.57, bf16[1152]{0:T(1024)(128)(2,1)S(1)} %pad.1.clone), kind=kOutput, calls=%fused_computation.7 | convolution fusion | flops 2423783424 | bytes 11016448 | tf_op jit(solution)/shard_map/dot_general | solution.py:83
  129.0 1.8 dynamic-slice_bitcast_fusion
  130.8 1.0 copy-done
  131.8 1.9 collective-permute-start
  133.7 4.7 %collective-permute-done = f32[16,32,1152]{2,1,0:T(8,128)S(1)} collective-permute-done((f32[16,32,1152]{2,1,0:T(8,128)}, f32[16,32,1152]{2,1,0:T(8,128)S(1)}, u32[]{:S(2)}, u32[]{:S(2)}) %collective-permute-start) | collective-permute-done | bytes 2359328 | tf_op jit(solution)/shard_map/ppermute | solution.py:91
  138.4 3.4 %bitcast_add_fusion = f32[16,32,1152]{2,1,0:T(8,128)} fusion(f32[16,32,1152]{2,1,0:T(8,128)S(1)} %collective-permute-done, f32[16,2,32,1152]{3,2,1,0:T(8,128)} %bitcast.32, s32[]{:T(128)S(6)} %select_n.40), kind=kLoop, calls=%fused_computation.10 | loop fusion | flops 589824 | bytes 7077892 | tf_op jit(solution)/shard_map/add | solution.py:91
  141.8 68.8 %reduce-scatter.2.cloned.1.call-done = f32[1,32,1152]{2,1,0:T(8,128)} async-done(((f32[16,32,1152]{2,1,0:T(8,128)}), f32[1,32,1152]{2,1,0:T(8,128)}) %reduce-scatter.2.cloned.1.call-update) | async-done | bytes 147472 | tf_op jit(solution)/shard_map/reduce_scatter | solution.py:92
  210.6 0.8 fusion.10
  211.5 1.6 fusion.9
  (59 shorter events, 7.8 us)
Async XLA Ops:
  6.5 79.2 %all-gather.2.cloned.1.call-start = ((), (), s32[]{:S(2)}) async-start(), calls=%async_computation.4 | async-start | bytes 2162688 | tf_op jit(solution)/shard_map/all_gather | solution.py:53
  13.4 9.5 %copy-start.2 = (s32[8,3]{0,1:T(4,128)S(1)}, s32[8,3]{0,1:T(4,128)}, u32[]{:S(2)}) copy-start(s32[8,3]{0,1:T(4,128)} %param.5) | copy-start | bytes 292
  13.4 33.5 %all-to-all-start = ((bf16[16,64,1024]{2,1,0:T(8,128)(2,1)}), bf16[16,64,1024]{2,1,0:T(8,128)(2,1)S(1)}, u32[]{:S(2)}, u32[]{:S(2)}) async-start(bf16[16,64,1024]{2,1,0:T(8,128)(2,1)} %reshape.120), calls=%async_computation | async-start | bytes 4194304 | tf_op jit(solution)/shard_map/all_to_all | solution.py:48
  22.9 1.2 copy-start.3
  95.4 12.8 %all-to-all-start.1 = ((f32[16,1,128]{2,1,0:T(1,128)}), f32[16,1,128]{2,1,0:T(1,128)S(1)}, u32[]{:S(2)}, u32[]{:S(2)}) async-start(f32[16,1,128]{2,1,0:T(1,128)} %reshape.177), calls=%async_computation.1 | async-start | bytes 16384 | tf_op jit(solution)/shard_map/all_to_all | solution.py:64
  111.9 10.9 %all-to-all-start.2 = ((f32[16,1,64]{2,1,0:T(1,128)}), f32[16,1,64]{2,1,0:T(1,128)S(1)}, u32[]{:S(2)}, u32[]{:S(2)}) async-start(f32[16,1,64]{2,1,0:T(1,128)} %bitcast.7), calls=%async_computation.2 | async-start | bytes 16384 | tf_op jit(solution)/shard_map/all_to_all | solution.py:74
  117.2 93.4 %reduce-scatter.2.cloned.1.call-start = ((), (), s32[]{:S(2)}) async-start(), calls=%async_computation.5 | async-start | bytes 2506752 | tf_op jit(solution)/shard_map/reduce_scatter | solution.py:92
  129.0 2.8 %copy-start = (f32[1024,1152]{1,0:T(8,128)}, f32[1024,1152]{1,0:T(8,128)S(1)}, u32[]{:S(2)}) copy-start(f32[1024,1152]{1,0:T(8,128)S(1)} %fusion) | copy-start | bytes 14155780
  131.8 6.6 %collective-permute-start = (f32[16,32,1152]{2,1,0:T(8,128)}, f32[16,32,1152]{2,1,0:T(8,128)S(1)}, u32[]{:S(2)}, u32[]{:S(2)}) collective-permute-start(f32[16,32,1152]{2,1,0:T(8,128)} %dynamic-slice_bitcast_fusion), channel_id=1, source_target_pairs={{0,16},{16,0},{1,17},{17,1},{2,18},{18,2},{3,19},{19,3},{4,20},{20... | collective-permute-start | bytes 7077896 | tf_op jit(solution)/shard_map/ppermute | solution.py:91
  141.8 69.7 %copy-start.1 = (bf16[1,32,1024]{2,1,0:T(8,128)(2,1)S(1)}, bf16[1,32,1024]{2,1,0:T(8,128)(2,1)}, u32[]{:S(2)}) copy-start(bf16[1,32,1024]{2,1,0:T(8,128)(2,1)} %param.7) | copy-start | bytes 196612
Sparse Core Ops, SparseCore 0:
  9.5 76.2 all-gather.1
  142.0 68.6 reduce-scatter.1

commit v3 on v2

--- a/solution.py
+++ b/solution.py
@@ -80,15 +80,18 @@
     widened = jnp.concatenate(
         [incoming, jnp.broadcast_to(marker[None, :], (incoming.shape[0], 128))], axis=1
     )
-    block_sums = lax.dot_general(
-        shares, widened, (((0,), (0,)), ((), ())), preferred_element_type=jnp.float32
-    )
     n_core = lax.axis_size("core")
     core = lax.axis_index("core")
-    by_owner = block_sums.reshape(lax.axis_size("z"), n_core, -1, block_sums.shape[1])
-    mine = lax.dynamic_index_in_dim(by_owner, core, axis=1, keepdims=False)
-    other = lax.dynamic_index_in_dim(by_owner, n_core - 1 - core, axis=1, keepdims=False)
-    paired = mine + lax.ppermute(other, "core", [(0, 1), (1, 0)])
+    by_owner = shares.reshape(shares.shape[0], lax.axis_size("z"), n_core, -1)
+
+    def owner_sums(which):
+        picked = lax.dynamic_index_in_dim(by_owner, which, axis=2, keepdims=False)
+        return lax.dot_general(
+            picked, widened, (((0,), (0,)), ((), ())), preferred_element_type=jnp.float32
+        )
+
+    sent = lax.ppermute(owner_sums(n_core - 1 - core), "core", [(0, 1), (1, 0)])
+    paired = lax.optimization_barrier(owner_sums(core)) + sent
     reduced = lax.psum_scatter(paired, "z", scatter_dimension=0, tiled=True)[0]
     new_sums = reduced[:, :width]
     new_mass = reduced[:, width]

time: 221 us -> 217 us (0.982)
  waiting for transfers between devices: 146 us -> 143 us
  local copies, waits for them, and re-layouts: 12.2 us -> 9.45 us
    ppermute x1, waiting for transfers between devices: 4.71 us -> 1.24 us  [per_device(): sent = lax.ppermute(owner_sums(n_core - 1 - core), 'core', [(0, 1), (1, 0)])]
    convert_element_type x0 -> x1, other arithmetic: none -> 2.83 us  [per_device(): shares = jnp.exp(logits - row_norms[:, None]).astype(jnp.bfloat16)]
    dot_general x1 -> x2, matrix products: 4.97 us -> 6.45 us  [owner_sums(): lax.dot_general(picked, widened, (((0,), (0,)), ((), ())), preferred_elem...]
  transfers between devices with their start and end apart: 6 -> 6, of which waited for: 6 -> 6; matrix products, arithmetic and copies ran while one was open for 4% -> 5% of each run, Pallas kernels for 0% -> 0%
where the time goes in v3:
time: 217 us; the launch traced here: 216 us
  waiting for transfers between devices  143 us (66%)
  starting transfers between devices  24 us (11%)
  between operations  13.6 us (6%)
  other arithmetic  13.3 us (6%)
  matrix products  13.2 us (6%)
  local copies, waits for them, and re-layouts  9.45 us (4%)
    reduce_scatter x1, waiting for transfers between devices, per_device(): reduced = lax.psum_scatter(paired, 'z', scatter_dimension=0, tiled=True)[0]  68.8 us
    all_gather x1, waiting for transfers between devices, per_device(): lax.all_gather(centroids, ('z', 'core'), axis=1, tiled=True)[0]  38.8 us
    all_to_all x1, waiting for transfers between devices, per_device(): lax.all_to_all(outgoing, 'cent', split_axis=0, concat_axis=0, tiled=True)  22.5 us
    all_to_all x1, starting transfers between devices, per_device(): lax.all_to_all(outgoing, 'cent', split_axis=0, concat_axis=0, tiled=True)  9.5 us
    all_to_all x1, starting transfers between devices, per_device(): lax.all_to_all(stats, 'cent', split_axis=0, concat_axis=0, tiled=True)  7.26 us
    dot_general x2, matrix products, owner_sums(): lax.dot_general(picked, widened, (((0,), (0,)), ((), ())), preferred_elem...  6.45 us
    dot_general x1, matrix products, per_device(): lax.dot_general(incoming, lax.all_gather(centroids, ('z', 'core'), axis=1...  5.89 us
    all_to_all x1, waiting for transfers between devices, per_device(): lax.all_to_all(slot_norms.reshape(owners, slot_rows), 'cent', split_axis=...  5.48 us
  transfers between devices with their start and end apart: 6, of which 6 were waited for; matrix products, arithmetic and copies ran while one was open for 5% of the time, Pallas kernels for 0%

profile of v3, /device:TPU:6, one launch (start us, length us, event | category | flops | bytes accessed | tf_op | source)
XLA Modules:
  0.0 216.4 jit_solution(14620073997949595513)
XLA Ops:
  6.5 0.7 all-gather.2.cloned.1.call-update
  7.3 0.7 iota_compare_fusion.1
  8.1 0.8 fusion.18
  9.1 1.3 reshape.119
  11.0 2.4 %reshape.120 = bf16[16,64,1024]{2,1,0:T(8,128)(2,1)} reshape(bf16[32,32768]{1,0:T(8,128)(2,1)S(1)} %convolution_convert_fusion) | data formatting | bytes 4194304 | tf_op jit(solution)/shard_map/reshape | solution.py:47
  13.4 9.5 %all-to-all-start = ((bf16[16,64,1024]{2,1,0:T(8,128)(2,1)}), bf16[16,64,1024]{2,1,0:T(8,128)(2,1)S(1)}, u32[]{:S(2)}, u32[]{:S(2)}) async-start(bf16[16,64,1024]{2,1,0:T(8,128)(2,1)} %reshape.120), calls=%async_computation | async-start | bytes 4194304 | tf_op jit(solution)/shard_map/all_to_all | solution.py:48
  23.3 0.7 gather_fusion.2
  24.4 22.5 %all-to-all-done = bf16[16,64,1024]{2,1,0:T(8,128)(2,1)S(1)} async-done(((bf16[16,64,1024]{2,1,0:T(8,128)(2,1)}), bf16[16,64,1024]{2,1,0:T(8,128)(2,1)S(1)}, u32[]{:S(2)}, u32[]{:S(2)}) %all-to-all-start) | async-done | bytes 2097184 | tf_op jit(solution)/shard_map/all_to_all | solution.py:48
  46.9 38.8 %all-gather.2.cloned.1.call-done = bf16[1,1024,1024]{2,1,0:T(8,128)(2,1)} async-done(((bf16[1,32,1024]{2,1,0:T(8,128)(2,1)}), bf16[1,1024,1024]{2,1,0:T(8,128)(2,1)}) %all-gather.2.cloned.1.call-update) | async-done | bytes 2097168 | tf_op jit(solution)/shard_map/all_gather | solution.py:53
  85.7 5.9 %multiply_reduce_fusion = (f32[1024]{0:T(1024)S(1)}, f32[1024,1024]{0,1:T(8,128)}) fusion(bf16[1024,1024]{1,0:T(8,128)(2,1)S(1)} %bitcast.37, bf16[1,1024,1024]{2,1,0:T(8,128)(2,1)} %all-gather.2.cloned.1.call-done), kind=kOutput, calls=%fused_computation.6 | convolution fusion | flops 2149579776 | bytes 8392704 | tf_op jit(solution)/shard_map/dot_general | solution.py:51
  91.7 2.9 %exponential_reduce_fusion = f32[1024]{0:T(1024)S(1)} fusion(f32[1024,1024]{0,1:T(8,128)} %get-tuple-element.10, f32[1024]{0:T(1024)S(1)} %get-tuple-element.9), kind=kLoop, calls=%fused_computation.5 | loop fusion | flops 3144704 | bytes 4202496 | tf_op jit(solution)/shard_map/reduce_sum | solution.py:60
  95.4 7.3 %all-to-all-start.1 = ((f32[16,1,128]{2,1,0:T(1,128)}), f32[16,1,128]{2,1,0:T(1,128)S(1)}, u32[]{:S(2)}, u32[]{:S(2)}) async-start(f32[16,1,128]{2,1,0:T(1,128)} %reshape.178), calls=%async_computation.1 | async-start | bytes 16384 | tf_op jit(solution)/shard_map/all_to_all | solution.py:64
  102.9 5.3 %all-to-all-done.1 = f32[16,1,128]{2,1,0:T(1,128)S(1)} async-done(((f32[16,1,128]{2,1,0:T(1,128)}), f32[16,1,128]{2,1,0:T(1,128)S(1)}, u32[]{:S(2)}, u32[]{:S(2)}) %all-to-all-start.1) | async-done | bytes 8224 | tf_op jit(solution)/shard_map/all_to_all | solution.py:64
  111.9 5.3 %all-to-all-start.2 = ((f32[16,1,64]{2,1,0:T(1,128)}), f32[16,1,64]{2,1,0:T(1,128)S(1)}, u32[]{:S(2)}, u32[]{:S(2)}) async-start(f32[16,1,64]{2,1,0:T(1,128)} %bitcast.7), calls=%async_computation.2 | async-start | bytes 16384 | tf_op jit(solution)/shard_map/all_to_all | solution.py:74
  117.3 5.5 %all-to-all-done.2 = f32[16,1,64]{2,1,0:T(1,128)S(1)} async-done(((f32[16,1,64]{2,1,0:T(1,128)}), f32[16,1,64]{2,1,0:T(1,128)S(1)}, u32[]{:S(2)}, u32[]{:S(2)}) %all-to-all-start.2) | async-done | bytes 4128 | tf_op jit(solution)/shard_map/all_to_all | solution.py:74
  124.0 2.8 %exponential_convert_fusion = bf16[1024,1024]{0,1:T(8,128)(2,1)S(1)} fusion(f32[1024,1024]{0,1:T(8,128)} %get-tuple-element.10, f32[1024]{0:T(1024)S(1)} %sub.57), kind=kLoop, calls=%fused_computation.4 | loop fusion | flops 3145728 | bytes 6295552 | tf_op jit(solution)/shard_map/convert_element_type | solution.py:77
  126.9 3.0 %fusion.2 = f32[16,32,1152]{2,1,0:T(8,128)} fusion(bf16[1024,1024]{1,0:T(8,128)(2,1)S(1)} %bitcast.38, bf16[1152]{0:T(1024)(128)(2,1)S(1)} %pad.1.clone, bf16[1024,16,2,32]{0,3,2,1:T(8,128)(2,1)S(1)} %bitcast.40, s32[]{:T(128)S(6)} %select_n.41), kind=kOutput, calls=%fused_computation.10 | convolution fusion | flops 1212678144 | bytes 5509124 | tf_op jit(solution)/shard_map/dot_general | solution.py:89
  129.9 1.9 collective-permute-start
  131.8 3.5 %fusion.3 = f32[16,32,1152]{2,1,0:T(8,128)S(1)} fusion(bf16[1024,1024]{1,0:T(8,128)(2,1)} %bitcast.39, bf16[1152]{0:T(1024)(128)(2,1)S(1)} %pad.1.clone, bf16[1024,16,2,32]{0,3,2,1:T(8,128)(2,1)} %bitcast.41, s32[]{:T(128)S(6)} %select_n.40), kind=kOutput, calls=%fused_computation.11 | convolution fusion | flops 1212678144 | bytes 5507332 | tf_op jit(solution)/shard_map/dot_general | solution.py:89
  135.3 1.2 collective-permute-done
  136.5 1.7 add.50
  138.3 68.8 %reduce-scatter.2.cloned.1.call-done = f32[1,32,1152]{2,1,0:T(8,128)} async-done(((f32[16,32,1152]{2,1,0:T(8,128)}), f32[1,32,1152]{2,1,0:T(8,128)}) %reduce-scatter.2.cloned.1.call-update) | async-done | bytes 147472 | tf_op jit(solution)/shard_map/reduce_scatter | solution.py:95
  207.1 0.8 fusion.12
  207.9 1.6 fusion.11
  (62 shorter events, 7.8 us)
Async XLA Ops:
  6.5 79.2 %all-gather.2.cloned.1.call-start = ((), (), s32[]{:S(2)}) async-start(), calls=%async_computation.4 | async-start | bytes 2162688 | tf_op jit(solution)/shard_map/all_gather | solution.py:53
  13.4 9.5 %copy-start.3 = (s32[8,3]{0,1:T(4,128)S(1)}, s32[8,3]{0,1:T(4,128)}, u32[]{:S(2)}) copy-start(s32[8,3]{0,1:T(4,128)} %param.5) | copy-start | bytes 292
  13.4 33.4 %all-to-all-start = ((bf16[16,64,1024]{2,1,0:T(8,128)(2,1)}), bf16[16,64,1024]{2,1,0:T(8,128)(2,1)S(1)}, u32[]{:S(2)}, u32[]{:S(2)}) async-start(bf16[16,64,1024]{2,1,0:T(8,128)(2,1)} %reshape.120), calls=%async_computation | async-start | bytes 4194304 | tf_op jit(solution)/shard_map/all_to_all | solution.py:48
  22.9 1.2 copy-start.4
  46.9 80.0 %copy-start = (bf16[16,64,1024]{2,1,0:T(8,128)(2,1)}, bf16[16,64,1024]{2,1,0:T(8,128)(2,1)S(1)}, u32[]{:S(2)}) copy-start(bf16[16,64,1024]{2,1,0:T(8,128)(2,1)S(1)} %all-to-all-done) | copy-start | bytes 6291460
  95.4 12.8 %all-to-all-start.1 = ((f32[16,1,128]{2,1,0:T(1,128)}), f32[16,1,128]{2,1,0:T(1,128)S(1)}, u32[]{:S(2)}, u32[]{:S(2)}) async-start(f32[16,1,128]{2,1,0:T(1,128)} %reshape.178), calls=%async_computation.1 | async-start | bytes 16384 | tf_op jit(solution)/shard_map/all_to_all | solution.py:64
  111.9 10.9 %all-to-all-start.2 = ((f32[16,1,64]{2,1,0:T(1,128)}), f32[16,1,64]{2,1,0:T(1,128)S(1)}, u32[]{:S(2)}, u32[]{:S(2)}) async-start(f32[16,1,64]{2,1,0:T(1,128)} %bitcast.7), calls=%async_computation.2 | async-start | bytes 16384 | tf_op jit(solution)/shard_map/all_to_all | solution.py:74
  117.2 89.9 %reduce-scatter.2.cloned.1.call-start = ((), (), s32[]{:S(2)}) async-start(), calls=%async_computation.5 | async-start | bytes 2506752 | tf_op jit(solution)/shard_map/reduce_scatter | solution.py:95
  126.9 3.0 %copy-start.1 = (bf16[1024,1024]{0,1:T(8,128)(2,1)}, bf16[1024,1024]{0,1:T(8,128)(2,1)S(1)}, u32[]{:S(2)}) copy-start(bf16[1024,1024]{0,1:T(8,128)(2,1)S(1)} %exponential_convert_fusion) | copy-start | bytes 6291460
  129.9 6.6 %collective-permute-start = (f32[16,32,1152]{2,1,0:T(8,128)}, f32[16,32,1152]{2,1,0:T(8,128)S(1)}, u32[]{:S(2)}, u32[]{:S(2)}) collective-permute-start(f32[16,32,1152]{2,1,0:T(8,128)} %fusion.2), channel_id=1, source_target_pairs={{0,16},{16,0},{1,17},{17,1},{2,18},{18,2},{3,19},{19,3},{4,20},{20... | collective-permute-start | bytes 7077896 | tf_op jit(solution)/shard_map/ppermute | solution.py:93
  138.2 69.7 %copy-start.2 = (bf16[1,32,1024]{2,1,0:T(8,128)(2,1)S(1)}, bf16[1,32,1024]{2,1,0:T(8,128)(2,1)}, u32[]{:S(2)}) copy-start(bf16[1,32,1024]{2,1,0:T(8,128)(2,1)} %param.7) | copy-start | bytes 196612
Sparse Core Ops, SparseCore 0:
  9.5 76.2 all-gather.1
  138.4 68.6 reduce-scatter.1

commit v4 on v3

--- a/solution.py
+++ b/solution.py
@@ -45,7 +45,13 @@
         preferred_element_type=jnp.float32,
     )
     outgoing = outgoing.astype(jnp.bfloat16).reshape(owners, slot_rows, width)
+    slot_routes = (
+        jnp.dot(placing, (route_code + 1).astype(jnp.float32), precision=lax.Precision.HIGHEST)
+        - 1.0
+    )
+    slot_routes = jnp.round(slot_routes).astype(jnp.int32).reshape(owners, capacity, listed)
     arrived = lax.all_to_all(outgoing, "cent", split_axis=0, concat_axis=0, tiled=True)
+    arrived_routes = lax.all_to_all(slot_routes, "cent", split_axis=0, concat_axis=0, tiled=True)
     incoming = arrived.reshape(owners * slot_rows, width)
     logits = (
         lax.dot_general(
@@ -58,22 +64,17 @@
     )
     peaks = jnp.max(logits, axis=1)
     totals = jnp.sum(jnp.exp(logits - peaks[:, None]), axis=1)
-    stats = jnp.stack(
-        [peaks.reshape(owners, slot_rows), totals.reshape(owners, slot_rows)], axis=1
+    every = lax.all_gather(jnp.stack([peaks, totals]), "cent", axis=0, tiled=False)
+    every = every.reshape(owners, 2, owners, capacity, tile_rows)
+    held = arrived_routes >= 0
+    code = jnp.maximum(arrived_routes, 0)
+    source = jnp.arange(owners, dtype=jnp.int32)[:, None, None]
+    slot_norms = combine_norms(
+        every[code // capacity, 0, source, code % capacity],
+        every[code // capacity, 1, source, code % capacity],
+        held,
     )
-    back = lax.all_to_all(stats, "cent", split_axis=0, concat_axis=0, tiled=True)
-    back_peaks = back[:, 0].reshape(owners * capacity, tile_rows)
-    back_totals = back[:, 1].reshape(owners * capacity, tile_rows)
-    lookup = jnp.where(usable, route_code, 0)
-    tile_norms = combine_norms(back_peaks[lookup], back_totals[lookup], usable)
-    empty = 1.0 - jnp.sum(placing, axis=1)
-    slot_norms = (
-        jnp.dot(placing, tile_norms, precision=lax.Precision.HIGHEST)
-        + empty[:, None] * empty_norm
-    )
-    row_norms = lax.all_to_all(
-        slot_norms.reshape(owners, slot_rows), "cent", split_axis=0, concat_axis=0, tiled=True
-    ).reshape(-1)
+    row_norms = jnp.where(jnp.any(held, axis=-1)[..., None], slot_norms, empty_norm).reshape(-1)
     shares = jnp.exp(logits - row_norms[:, None]).astype(jnp.bfloat16)
     own_rows = centroids[0].astype(jnp.float32)
     marker = (jnp.arange(128, dtype=jnp.int32) == 0).astype(jnp.bfloat16)

time: 217 us -> 213 us (0.982)
  blocking collectives: 0 us -> 23.4 us
  waiting for transfers between devices: 143 us -> 126 us
  starting transfers between devices: 24 us -> 16.7 us
  other arithmetic: 13.3 us -> 10.2 us
    all_gather x0 -> x1, blocking collectives: none -> 23.4 us  [per_device(): lax.all_gather(jnp.stack([peaks, totals]), 'cent', axis=0, tiled=False)]
    all_gather x1, waiting for transfers between devices: 38.8 us -> 30.3 us  [per_device(): lax.all_gather(centroids, ('z', 'core'), axis=1, tiled=True)[0]]
    all_to_all x2 -> x1, waiting for transfers between devices: 10.8 us -> 2.32 us  [per_device(): lax.all_to_all(slot_routes, 'cent', split_axis=0, concat_axis=0, tiled=True)]
    all_to_all x1, starting transfers between devices: 9.5 us -> 5.58 us  [per_device(): lax.all_to_all(outgoing, 'cent', split_axis=0, concat_axis=0, tiled=True)]
    all_to_all x2 -> x1, starting transfers between devices: 12.6 us -> 9.15 us  [per_device(): lax.all_to_all(slot_routes, 'cent', split_axis=0, concat_axis=0, tiled=True)]
    reduce_sum x1, other arithmetic: 2.92 us -> 0.73 us  [per_device(): totals = jnp.sum(jnp.exp(logits - peaks[:, None]), axis=1)]
  transfers between devices with their start and end apart: 6 -> 5, of which waited for: 6 -> 5; matrix products, arithmetic and copies ran while one was open for 5% -> 6% of each run, Pallas kernels for 0% -> 0%
where the time goes in v4:
time: 213 us; the launch traced here: 212 us
  waiting for transfers between devices  126 us (59%)
  blocking collectives  23.4 us (11%)
  starting transfers between devices  16.7 us (8%)
  between operations  13.6 us (6%)
  matrix products  11.3 us (5%)
  local copies, waits for them, and re-layouts  11.2 us (5%)
  other arithmetic  10.2 us (5%)
    reduce_scatter x1, waiting for transfers between devices, per_device(): reduced = lax.psum_scatter(paired, 'z', scatter_dimension=0, tiled=True)[0]  69.4 us
    all_gather x1, waiting for transfers between devices, per_device(): lax.all_gather(centroids, ('z', 'core'), axis=1, tiled=True)[0]  30.3 us
    all_gather x1, blocking collectives, per_device(): lax.all_gather(jnp.stack([peaks, totals]), 'cent', axis=0, tiled=False)  23.4 us
    all_to_all x1, waiting for transfers between devices, per_device(): lax.all_to_all(outgoing, 'cent', split_axis=0, concat_axis=0, tiled=True)  21.7 us
    all_to_all x1, starting transfers between devices, per_device(): lax.all_to_all(slot_routes, 'cent', split_axis=0, concat_axis=0, tiled=True)  9.15 us
    dot_general x2, matrix products, owner_sums(): lax.dot_general(picked, widened, (((0,), (0,)), ((), ())), preferred_elem...  6.43 us
    all_to_all x1, starting transfers between devices, per_device(): lax.all_to_all(outgoing, 'cent', split_axis=0, concat_axis=0, tiled=True)  5.58 us
  transfers between devices with their start and end apart: 5, of which 5 were waited for; matrix products, arithmetic and copies ran while one was open for 6% of the time, Pallas kernels for 0%

profile of v4, /device:TPU:6, one launch (start us, length us, event | category | flops | bytes accessed | tf_op | source)
XLA Modules:
  0.0 212.2 jit_solution(5729989448172911851)
XLA Ops:
  8.1 0.8 copy.50
  9.1 0.8 fusion.19
  10.0 0.7 gather_fusion.2
  12.0 9.1 %all-to-all-start.1 = ((s32[16,2,3]{2,1,0:T(2,128)}), s32[16,2,3]{2,1,0:T(2,128)S(1)}, u32[]{:S(2)}, u32[]{:S(2)}) async-start(s32[16,2,3]{2,1,0:T(2,128)} %bitcast.7), calls=%async_computation.1 | async-start | bytes 32768 | tf_op jit(solution)/shard_map/all_to_all | solution.py:54
  22.2 2.4 %reshape.128 = bf16[16,64,1024]{2,1,0:T(8,128)(2,1)} reshape(bf16[32,32768]{1,0:T(8,128)(2,1)S(1)} %convolution_convert_fusion) | data formatting | bytes 4194304 | tf_op jit(solution)/shard_map/reshape | solution.py:47
  24.5 2.3 %all-to-all-done.1 = s32[16,2,3]{2,1,0:T(2,128)S(1)} async-done(((s32[16,2,3]{2,1,0:T(2,128)}), s32[16,2,3]{2,1,0:T(2,128)S(1)}, u32[]{:S(2)}, u32[]{:S(2)}) %all-to-all-start.1) | async-done | bytes 416 | tf_op jit(solution)/shard_map/all_to_all | solution.py:54
  26.9 5.6 %all-to-all-start = ((bf16[16,64,1024]{2,1,0:T(8,128)(2,1)}), bf16[16,64,1024]{2,1,0:T(8,128)(2,1)S(1)}, u32[]{:S(2)}, u32[]{:S(2)}) async-start(bf16[16,64,1024]{2,1,0:T(8,128)(2,1)} %reshape.128), calls=%async_computation | async-start | bytes 4194304 | tf_op jit(solution)/shard_map/all_to_all | solution.py:53
  33.6 21.7 %all-to-all-done = bf16[16,64,1024]{2,1,0:T(8,128)(2,1)S(1)} async-done(((bf16[16,64,1024]{2,1,0:T(8,128)(2,1)}), bf16[16,64,1024]{2,1,0:T(8,128)(2,1)S(1)}, u32[]{:S(2)}, u32[]{:S(2)}) %all-to-all-start) | async-done | bytes 2097184 | tf_op jit(solution)/shard_map/all_to_all | solution.py:53
  55.3 30.3 %all-gather.4.cloned.1.call-done = bf16[1,1024,1024]{2,1,0:T(8,128)(2,1)} async-done(((bf16[1,32,1024]{2,1,0:T(8,128)(2,1)}), bf16[1,1024,1024]{2,1,0:T(8,128)(2,1)}) %all-gather.4.cloned.1.call-update) | async-done | bytes 2097168 | tf_op jit(solution)/shard_map/all_gather | solution.py:59
  85.7 4.0 %multiply_reduce_fusion = (f32[1024]{0:T(1024)S(1)}, f32[1024,1024]{0,1:T(8,128)S(1)}) fusion(bf16[1024,1024]{1,0:T(8,128)(2,1)S(1)} %bitcast.57, bf16[1,1024,1024]{2,1,0:T(8,128)(2,1)} %all-gather.4.cloned.1.call-done), kind=kOutput, calls=%fused_computation.6 | convolution fusion | flops 2149579776 | bytes 8392704 | tf_op jit(solution)/shard_map/dot_general | solution.py:57
  89.6 2.0 copy-done
  91.7 0.7 exponential_reduce_fusion
  92.4 23.4 %all-gather.1 = f32[16,2,1024]{2,1,0:T(2,128)S(1)} all-gather(f32[1,2,1024]{2,1,0:T(2,128)S(1)} %maximum_bitcast_fusion.3), channel_id=2, replica_groups=mesh['z'=16,'core'=2,'cent'=16] {'cent'}, dimensions={0}, use_global_device_ids=true | all-gather | bytes 139264 | tf_op jit(solution)/shard_map/all_gather | solution.py:67
  116.3 1.2 gather_fusion.1
  117.5 1.2 gather_fusion
  119.2 2.8 %exponential_convert_fusion = bf16[1024,1024]{0,1:T(8,128)(2,1)S(1)} fusion(f32[1024,1024]{0,1:T(8,128)} %copy-done, f32[1024]{0:T(1024)S(1)} %select_n.72), kind=kLoop, calls=%fused_computation.4 | loop fusion | flops 3145728 | bytes 6295552 | tf_op jit(solution)/shard_map/convert_element_type | solution.py:78
  122.1 3.0 %fusion.2 = f32[16,32,1152]{2,1,0:T(8,128)} fusion(bf16[1024,1024]{1,0:T(8,128)(2,1)S(1)} %bitcast.58, bf16[1152]{0:T(1024)(128)(2,1)S(1)} %pad.1.clone, bf16[1024,16,2,32]{0,3,2,1:T(8,128)(2,1)S(1)} %bitcast.60, s32[]{:T(128)S(6)} %select_n.74), kind=kOutput, calls=%fused_computation.10 | convolution fusion | flops 1212678144 | bytes 5509124 | tf_op jit(solution)/shard_map/dot_general | solution.py:90
  125.1 1.9 collective-permute-start
  127.0 3.5 %fusion.3 = f32[16,32,1152]{2,1,0:T(8,128)S(1)} fusion(bf16[1024,1024]{1,0:T(8,128)(2,1)} %bitcast.59, bf16[1152]{0:T(1024)(128)(2,1)S(1)} %pad.1.clone, bf16[1024,16,2,32]{0,3,2,1:T(8,128)(2,1)} %bitcast.61, s32[]{:T(128)S(6)} %select_n.73), kind=kOutput, calls=%fused_computation.11 | convolution fusion | flops 1212678144 | bytes 5507332 | tf_op jit(solution)/shard_map/dot_general | solution.py:90
  130.5 1.2 collective-permute-done
  131.7 1.7 add.69
  133.5 69.4 %reduce-scatter.2.cloned.1.call-done = f32[1,32,1152]{2,1,0:T(8,128)} async-done(((f32[16,32,1152]{2,1,0:T(8,128)}), f32[1,32,1152]{2,1,0:T(8,128)}) %reduce-scatter.2.cloned.1.call-update) | async-done | bytes 147472 | tf_op jit(solution)/shard_map/reduce_scatter | solution.py:96
  202.9 0.8 fusion.15
  203.7 1.6 fusion.13
  (57 shorter events, 6.2 us)
Async XLA Ops:
  6.5 4.5 %copy-start.5 = (s32[8]{0:T(128)S(1)}, s32[8]{0:T(128)}, u32[]{:S(2)}) copy-start(s32[8]{0:T(128)} %param.6) | copy-start | bytes 100
  6.5 14.7 %copy-start.3 = (bf16[256,1024]{1,0:T(8,128)(2,1)S(1)}, bf16[256,1024]{1,0:T(8,128)(2,1)}, u32[]{:S(2)}) copy-start(bf16[256,1024]{1,0:T(8,128)(2,1)} %param.4) | copy-start | bytes 1572868
  6.5 79.1 %all-gather.4.cloned.1.call-start = ((), (), s32[]{:S(2)}) async-start(), calls=%async_computation.3 | async-start | bytes 2162688 | tf_op jit(solution)/shard_map/all_gather | solution.py:59
  12.0 14.8 %all-to-all-start.1 = ((s32[16,2,3]{2,1,0:T(2,128)}), s32[16,2,3]{2,1,0:T(2,128)S(1)}, u32[]{:S(2)}, u32[]{:S(2)}) async-start(s32[16,2,3]{2,1,0:T(2,128)} %bitcast.7), calls=%async_computation.1 | async-start | bytes 32768 | tf_op jit(solution)/shard_map/all_to_all | solution.py:54
  26.9 28.5 %all-to-all-start = ((bf16[16,64,1024]{2,1,0:T(8,128)(2,1)}), bf16[16,64,1024]{2,1,0:T(8,128)(2,1)S(1)}, u32[]{:S(2)}, u32[]{:S(2)}) async-start(bf16[16,64,1024]{2,1,0:T(8,128)(2,1)} %reshape.128), calls=%async_computation | async-start | bytes 4194304 | tf_op jit(solution)/shard_map/all_to_all | solution.py:53
  32.4 170.5 %reduce-scatter.2.cloned.1.call-start = ((), (), s32[]{:S(2)}) async-start(), calls=%async_computation.4 | async-start | bytes 2506752 | tf_op jit(solution)/shard_map/reduce_scatter | solution.py:96
  55.3 66.8 %copy-start.1 = (bf16[16,64,1024]{2,1,0:T(8,128)(2,1)}, bf16[16,64,1024]{2,1,0:T(8,128)(2,1)S(1)}, u32[]{:S(2)}) copy-start(bf16[16,64,1024]{2,1,0:T(8,128)(2,1)S(1)} %all-to-all-done) | copy-start | bytes 6291460
  89.6 2.0 copy-start
  122.1 3.0 %copy-start.2 = (bf16[1024,1024]{0,1:T(8,128)(2,1)}, bf16[1024,1024]{0,1:T(8,128)(2,1)S(1)}, u32[]{:S(2)}) copy-start(bf16[1024,1024]{0,1:T(8,128)(2,1)S(1)} %exponential_convert_fusion) | copy-start | bytes 6291460
  125.1 6.6 %collective-permute-start = (f32[16,32,1152]{2,1,0:T(8,128)}, f32[16,32,1152]{2,1,0:T(8,128)S(1)}, u32[]{:S(2)}, u32[]{:S(2)}) collective-permute-start(f32[16,32,1152]{2,1,0:T(8,128)} %fusion.2), channel_id=1, source_target_pairs={{0,16},{16,0},{1,17},{17,1},{2,18},{18,2},{3,19},{19,3},{4,20},{20... | collective-permute-start | bytes 7077896 | tf_op jit(solution)/shard_map/ppermute | solution.py:94
  133.4 70.3 %copy-start.4 = (bf16[1,32,1024]{2,1,0:T(8,128)(2,1)S(1)}, bf16[1,32,1024]{2,1,0:T(8,128)(2,1)}, u32[]{:S(2)}) copy-start(bf16[1,32,1024]{2,1,0:T(8,128)(2,1)} %param.7) | copy-start | bytes 196612
Sparse Core Ops, SparseCore 0:
  9.5 76.1 all-gather.3
  133.6 69.2 reduce-scatter.1

commit v5 on v4

--- a/solution.py
+++ b/solution.py
@@ -64,7 +64,14 @@
     )
     peaks = jnp.max(logits, axis=1)
     totals = jnp.sum(jnp.exp(logits - peaks[:, None]), axis=1)
-    every = lax.all_gather(jnp.stack([peaks, totals]), "cent", axis=0, tiled=False)
+    stats = jnp.stack([peaks, totals])
+    every = lax.all_to_all(
+        jnp.broadcast_to(stats[None], (owners, *stats.shape)),
+        "cent",
+        split_axis=0,
+        concat_axis=0,
+        tiled=True,
+    )
     every = every.reshape(owners, 2, owners, capacity, tile_rows)
     held = arrived_routes >= 0
     code = jnp.maximum(arrived_routes, 0)

time: 213 us -> 203 us (0.953)
  blocking collectives: 23.4 us -> 0 us
  starting transfers between devices: 16.7 us -> 24.1 us
  waiting for transfers between devices: 126 us -> 131 us
    all_gather x1 -> x0, blocking collectives: 23.4 us -> none  [per_device(): lax.all_gather(jnp.stack([peaks, totals]), 'cent', axis=0, tiled=False)]
    all_to_all x0 -> x1, starting transfers between devices: none -> 7.44 us  [per_device(): lax.all_to_all(jnp.broadcast_to(stats[None], (owners, *stats.shape)), 'ce...]
    all_to_all x0 -> x1, waiting for transfers between devices: none -> 5.39 us  [per_device(): lax.all_to_all(jnp.broadcast_to(stats[None], (owners, *stats.shape)), 'ce...]
  transfers between devices with their start and end apart: 5 -> 6, of which waited for: 5 -> 6; matrix products, arithmetic and copies ran while one was open for 6% -> 6% of each run, Pallas kernels for 0% -> 0%
where the time goes in v5:
time: 203 us; the launch traced here: 202 us
  waiting for transfers between devices  131 us (65%)
  starting transfers between devices  24.1 us (12%)
  between operations  13.6 us (7%)
  local copies, waits for them, and re-layouts  11.9 us (6%)
  matrix products  11.3 us (6%)
  other arithmetic  10.2 us (5%)
    reduce_scatter x1, waiting for transfers between devices, per_device(): reduced = lax.psum_scatter(paired, 'z', scatter_dimension=0, tiled=True)[0]  69 us
    all_gather x1, waiting for transfers between devices, per_device(): lax.all_gather(centroids, ('z', 'core'), axis=1, tiled=True)[0]  30.3 us
    all_to_all x1, waiting for transfers between devices, per_device(): lax.all_to_all(outgoing, 'cent', split_axis=0, concat_axis=0, tiled=True)  22.2 us
    all_to_all x1, starting transfers between devices, per_device(): lax.all_to_all(slot_routes, 'cent', split_axis=0, concat_axis=0, tiled=True)  9.15 us
    all_to_all x1, starting transfers between devices, per_device(): lax.all_to_all(jnp.broadcast_to(stats[None], (owners, *stats.shape)), 'ce...  7.44 us
    dot_general x2, matrix products, owner_sums(): lax.dot_general(picked, widened, (((0,), (0,)), ((), ())), preferred_elem...  6.42 us
    all_to_all x1, starting transfers between devices, per_device(): lax.all_to_all(outgoing, 'cent', split_axis=0, concat_axis=0, tiled=True)  5.58 us
    all_to_all x1, waiting for transfers between devices, per_device(): lax.all_to_all(jnp.broadcast_to(stats[None], (owners, *stats.shape)), 'ce...  5.39 us
  transfers between devices with their start and end apart: 6, of which 6 were waited for; matrix products, arithmetic and copies ran while one was open for 6% of the time, Pallas kernels for 0%

profile of v5, /device:TPU:6, one launch (start us, length us, event | category | flops | bytes accessed | tf_op | source)
XLA Modules:
  0.0 202.3 jit_solution(16205388291375160663)
XLA Ops:
  8.1 0.8 copy.50
  9.1 0.8 fusion.19
  10.0 0.7 gather_fusion.2
  12.0 9.1 %all-to-all-start.1 = ((s32[16,2,3]{2,1,0:T(2,128)}), s32[16,2,3]{2,1,0:T(2,128)S(1)}, u32[]{:S(2)}, u32[]{:S(2)}) async-start(s32[16,2,3]{2,1,0:T(2,128)} %bitcast.7), calls=%async_computation.1 | async-start | bytes 32768 | tf_op jit(solution)/shard_map/all_to_all | solution.py:54
  22.2 2.4 %reshape.129 = bf16[16,64,1024]{2,1,0:T(8,128)(2,1)} reshape(bf16[32,32768]{1,0:T(8,128)(2,1)S(1)} %convolution_convert_fusion) | data formatting | bytes 4194304 | tf_op jit(solution)/shard_map/reshape | solution.py:47
  24.5 2.3 %all-to-all-done.1 = s32[16,2,3]{2,1,0:T(2,128)S(1)} async-done(((s32[16,2,3]{2,1,0:T(2,128)}), s32[16,2,3]{2,1,0:T(2,128)S(1)}, u32[]{:S(2)}, u32[]{:S(2)}) %all-to-all-start.1) | async-done | bytes 416 | tf_op jit(solution)/shard_map/all_to_all | solution.py:54
  26.9 5.6 %all-to-all-start = ((bf16[16,64,1024]{2,1,0:T(8,128)(2,1)}), bf16[16,64,1024]{2,1,0:T(8,128)(2,1)S(1)}, u32[]{:S(2)}, u32[]{:S(2)}) async-start(bf16[16,64,1024]{2,1,0:T(8,128)(2,1)} %reshape.129), calls=%async_computation | async-start | bytes 4194304 | tf_op jit(solution)/shard_map/all_to_all | solution.py:53
  33.2 22.2 %all-to-all-done = bf16[16,64,1024]{2,1,0:T(8,128)(2,1)S(1)} async-done(((bf16[16,64,1024]{2,1,0:T(8,128)(2,1)}), bf16[16,64,1024]{2,1,0:T(8,128)(2,1)S(1)}, u32[]{:S(2)}, u32[]{:S(2)}) %all-to-all-start) | async-done | bytes 2097184 | tf_op jit(solution)/shard_map/all_to_all | solution.py:53
  55.3 30.3 %all-gather.2.cloned.1.call-done = bf16[1,1024,1024]{2,1,0:T(8,128)(2,1)} async-done(((bf16[1,32,1024]{2,1,0:T(8,128)(2,1)}), bf16[1,1024,1024]{2,1,0:T(8,128)(2,1)}) %all-gather.2.cloned.1.call-update) | async-done | bytes 2097168 | tf_op jit(solution)/shard_map/all_gather | solution.py:59
  85.6 4.0 %multiply_reduce_fusion = (f32[1024]{0:T(1024)S(1)}, f32[1024,1024]{0,1:T(8,128)S(1)}) fusion(bf16[1024,1024]{1,0:T(8,128)(2,1)S(1)} %bitcast.55, bf16[1,1024,1024]{2,1,0:T(8,128)(2,1)} %all-gather.2.cloned.1.call-done), kind=kOutput, calls=%fused_computation.6 | convolution fusion | flops 2149579776 | bytes 8392704 | tf_op jit(solution)/shard_map/dot_general | solution.py:57
  89.6 2.0 %copy-done = f32[1024,1024]{0,1:T(8,128)} copy-done((f32[1024,1024]{0,1:T(8,128)}, f32[1024,1024]{0,1:T(8,128)S(1)}, u32[]{:S(2)}) %copy-start) | copy-done | bytes 4194328
  93.1 7.4 %all-to-all-start.2 = ((f32[16,2,1024]{2,1,0:T(2,128)}), f32[16,2,1024]{2,1,0:T(2,128)S(1)}, u32[]{:S(2)}, u32[]{:S(2)}) async-start(f32[16,2,1024]{2,1,0:T(2,128)} %broadcast_in_dim.89), calls=%async_computation.2 | async-start | bytes 262144 | tf_op jit(solution)/shard_map/all_to_all | solution.py:68
  100.9 5.4 %all-to-all-done.2 = f32[16,2,1024]{2,1,0:T(2,128)S(1)} async-done(((f32[16,2,1024]{2,1,0:T(2,128)}), f32[16,2,1024]{2,1,0:T(2,128)S(1)}, u32[]{:S(2)}, u32[]{:S(2)}) %all-to-all-start.2) | async-done | bytes 131104 | tf_op jit(solution)/shard_map/all_to_all | solution.py:68
  106.8 1.2 gather_fusion.1
  108.0 1.2 gather_fusion
  109.7 2.8 %exponential_convert_fusion = bf16[1024,1024]{0,1:T(8,128)(2,1)S(1)} fusion(f32[1024,1024]{0,1:T(8,128)} %copy-done, f32[1024]{0:T(1024)S(1)} %select_n.72), kind=kLoop, calls=%fused_computation.4 | loop fusion | flops 3145728 | bytes 6295552 | tf_op jit(solution)/shard_map/convert_element_type | solution.py:85
  112.6 3.0 %fusion.2 = f32[16,32,1152]{2,1,0:T(8,128)} fusion(bf16[1024,1024]{1,0:T(8,128)(2,1)S(1)} %bitcast.56, bf16[1152]{0:T(1024)(128)(2,1)S(1)} %pad.1.clone, bf16[1024,16,2,32]{0,3,2,1:T(8,128)(2,1)S(1)} %bitcast.58, s32[]{:T(128)S(6)} %select_n.74), kind=kOutput, calls=%fused_computation.10 | convolution fusion | flops 1212678144 | bytes 5509124 | tf_op jit(solution)/shard_map/dot_general | solution.py:97
  115.6 1.9 collective-permute-start
  117.5 3.5 %fusion.3 = f32[16,32,1152]{2,1,0:T(8,128)S(1)} fusion(bf16[1024,1024]{1,0:T(8,128)(2,1)} %bitcast.57, bf16[1152]{0:T(1024)(128)(2,1)S(1)} %pad.1.clone, bf16[1024,16,2,32]{0,3,2,1:T(8,128)(2,1)} %bitcast.59, s32[]{:T(128)S(6)} %select_n.73), kind=kOutput, calls=%fused_computation.11 | convolution fusion | flops 1212678144 | bytes 5507332 | tf_op jit(solution)/shard_map/dot_general | solution.py:97
  120.9 1.2 collective-permute-done
  122.2 1.7 add.69
  124.0 69.0 %reduce-scatter.2.cloned.1.call-done = f32[1,32,1152]{2,1,0:T(8,128)} async-done(((f32[16,32,1152]{2,1,0:T(8,128)}), f32[1,32,1152]{2,1,0:T(8,128)}) %reduce-scatter.2.cloned.1.call-update) | async-done | bytes 147472 | tf_op jit(solution)/shard_map/reduce_scatter | solution.py:103
  193.0 0.8 fusion.15
  193.8 1.6 fusion.13
  (59 shorter events, 7.6 us)
Async XLA Ops:
  6.5 4.5 %copy-start.5 = (s32[8]{0:T(128)S(1)}, s32[8]{0:T(128)}, u32[]{:S(2)}) copy-start(s32[8]{0:T(128)} %param.6) | copy-start | bytes 100
  6.5 14.7 %copy-start.3 = (bf16[256,1024]{1,0:T(8,128)(2,1)S(1)}, bf16[256,1024]{1,0:T(8,128)(2,1)}, u32[]{:S(2)}) copy-start(bf16[256,1024]{1,0:T(8,128)(2,1)} %param.4) | copy-start | bytes 1572868
  6.5 79.1 %all-gather.2.cloned.1.call-start = ((), (), s32[]{:S(2)}) async-start(), calls=%async_computation.4 | async-start | bytes 2162688 | tf_op jit(solution)/shard_map/all_gather | solution.py:59
  12.0 14.8 %all-to-all-start.1 = ((s32[16,2,3]{2,1,0:T(2,128)}), s32[16,2,3]{2,1,0:T(2,128)S(1)}, u32[]{:S(2)}, u32[]{:S(2)}) async-start(s32[16,2,3]{2,1,0:T(2,128)} %bitcast.7), calls=%async_computation.1 | async-start | bytes 32768 | tf_op jit(solution)/shard_map/all_to_all | solution.py:54
  26.9 28.5 %all-to-all-start = ((bf16[16,64,1024]{2,1,0:T(8,128)(2,1)}), bf16[16,64,1024]{2,1,0:T(8,128)(2,1)S(1)}, u32[]{:S(2)}, u32[]{:S(2)}) async-start(bf16[16,64,1024]{2,1,0:T(8,128)(2,1)} %reshape.129), calls=%async_computation | async-start | bytes 4194304 | tf_op jit(solution)/shard_map/all_to_all | solution.py:53
  55.3 57.3 %copy-start.1 = (bf16[16,64,1024]{2,1,0:T(8,128)(2,1)}, bf16[16,64,1024]{2,1,0:T(8,128)(2,1)S(1)}, u32[]{:S(2)}) copy-start(bf16[16,64,1024]{2,1,0:T(8,128)(2,1)S(1)} %all-to-all-done) | copy-start | bytes 6291460
  89.6 2.0 %copy-start = (f32[1024,1024]{0,1:T(8,128)}, f32[1024,1024]{0,1:T(8,128)S(1)}, u32[]{:S(2)}) copy-start(f32[1024,1024]{0,1:T(8,128)S(1)} %get-tuple-element.14) | copy-start | bytes 12582916
  93.1 13.2 %all-to-all-start.2 = ((f32[16,2,1024]{2,1,0:T(2,128)}), f32[16,2,1024]{2,1,0:T(2,128)S(1)}, u32[]{:S(2)}, u32[]{:S(2)}) async-start(f32[16,2,1024]{2,1,0:T(2,128)} %broadcast_in_dim.89), calls=%async_computation.2 | async-start | bytes 262144 | tf_op jit(solution)/shard_map/all_to_all | solution.py:68
  100.5 92.5 %reduce-scatter.2.cloned.1.call-start = ((), (), s32[]{:S(2)}) async-start(), calls=%async_computation.5 | async-start | bytes 2506752 | tf_op jit(solution)/shard_map/reduce_scatter | solution.py:103
  112.6 3.0 %copy-start.2 = (bf16[1024,1024]{0,1:T(8,128)(2,1)}, bf16[1024,1024]{0,1:T(8,128)(2,1)S(1)}, u32[]{:S(2)}) copy-start(bf16[1024,1024]{0,1:T(8,128)(2,1)S(1)} %exponential_convert_fusion) | copy-start | bytes 6291460
  115.6 6.6 %collective-permute-start = (f32[16,32,1152]{2,1,0:T(8,128)}, f32[16,32,1152]{2,1,0:T(8,128)S(1)}, u32[]{:S(2)}, u32[]{:S(2)}) collective-permute-start(f32[16,32,1152]{2,1,0:T(8,128)} %fusion.2), channel_id=1, source_target_pairs={{0,16},{16,0},{1,17},{17,1},{2,18},{18,2},{3,19},{19,3},{4,20},{20... | collective-permute-start | bytes 7077896 | tf_op jit(solution)/shard_map/ppermute | solution.py:101
  123.9 69.9 %copy-start.4 = (bf16[1,32,1024]{2,1,0:T(8,128)(2,1)S(1)}, bf16[1,32,1024]{2,1,0:T(8,128)(2,1)}, u32[]{:S(2)}) copy-start(bf16[1,32,1024]{2,1,0:T(8,128)(2,1)} %param.7) | copy-start | bytes 196612
Sparse Core Ops, SparseCore 0:
  9.5 76.1 all-gather.1
  124.1 68.8 reduce-scatter.1

commit v6 on v5

--- a/solution.py
+++ b/solution.py
@@ -15,6 +15,18 @@
     highest = jnp.max(jnp.where(keep, peaks, -1e30), axis=-2)
     summed = jnp.sum(jnp.where(keep, totals * jnp.exp(peaks - highest[..., None, :]), 0.0), axis=-2)
     return highest + jnp.log(summed)
+
+
+def gather_block(rows_here):
+    core = lax.axis_index("core")
+    high = lax.all_gather(rows_here, "zh", axis=0, tiled=True)
+    mine = lax.all_gather(high, "zl", axis=0, tiled=True)
+    other = lax.ppermute(mine, "core", [(0, 1), (1, 0)])
+    first = jnp.where(core == 0, mine, other)
+    second = jnp.where(core == 0, other, mine)
+    shape = (lax.axis_size("zl"), lax.axis_size("zh"), *rows_here.shape)
+    both = jnp.stack([first.reshape(shape), second.reshape(shape)], axis=2)
+    return both.transpose(1, 0, 2, 3, 4).reshape(-1, rows_here.shape[-1])
 
 
 def per_device(points, block_list, list_count, centroids):
@@ -56,7 +68,7 @@
     logits = (
         lax.dot_general(
             incoming,
-            lax.all_gather(centroids, ("z", "core"), axis=1, tiled=True)[0],
+            gather_block(centroids[0]),
             (((1,), (1,)), ((), ())),
             preferred_element_type=jnp.float32,
         )
@@ -90,7 +102,8 @@
     )
     n_core = lax.axis_size("core")
     core = lax.axis_index("core")
-    by_owner = shares.reshape(shares.shape[0], lax.axis_size("z"), n_core, -1)
+    n_z = lax.axis_size("zh") * lax.axis_size("zl")
+    by_owner = shares.reshape(shares.shape[0], n_z, n_core, -1)
 
     def owner_sums(which):
         picked = lax.dynamic_index_in_dim(by_owner, which, axis=2, keepdims=False)
@@ -100,7 +113,7 @@
 
     sent = lax.ppermute(owner_sums(n_core - 1 - core), "core", [(0, 1), (1, 0)])
     paired = lax.optimization_barrier(owner_sums(core)) + sent
-    reduced = lax.psum_scatter(paired, "z", scatter_dimension=0, tiled=True)[0]
+    reduced = lax.psum_scatter(paired, ("zh", "zl"), scatter_dimension=0, tiled=True)[0]
     new_sums = reduced[:, :width]
     new_mass = reduced[:, width]
     fresh = (new_sums + prior_weight * own_rows) / (new_mass[:, None] + prior_weight)
@@ -109,11 +122,13 @@
 
 def solution(mesh):
     cores = 2
+    low = 4
+    high = mesh.shape["dp"] // cores // low
     split = Mesh(
-        mesh.devices.reshape(mesh.shape["dp"] // cores, cores, mesh.shape["cent"]),
-        ("z", "core", "cent"),
+        mesh.devices.reshape(high, low, cores, mesh.shape["cent"]),
+        ("zh", "zl", "core", "cent"),
     )
-    rows = ("z", "core")
+    rows = ("zh", "zl", "core")
     in_specs = (
         P((*rows, "cent"), None),
         P((*rows, "cent"), None),

time: 203 us -> 198 us (0.975)
  waiting for transfers between devices: 131 us -> 93.1 us
  blocking collectives: 0 us -> 27.8 us
    all_gather x0 -> x1, blocking collectives: none -> 27.8 us  [gather_block(): high = lax.all_gather(rows_here, 'zh', axis=0, tiled=True)]
    all_to_all x1, waiting for transfers between devices: 22.2 us -> 2.68 us  [per_device(): lax.all_to_all(outgoing, 'cent', split_axis=0, concat_axis=0, tiled=True)]
    all_gather x1, waiting for transfers between devices: 30.3 us -> 11.3 us  [gather_block(): mine = lax.all_gather(high, 'zl', axis=0, tiled=True)]
    ppermute x0 -> x1, waiting for transfers between devices: none -> 2.09 us  [gather_block(): other = lax.ppermute(mine, 'core', [(0, 1), (1, 0)])]
  transfers between devices with their start and end apart: 6 -> 7, of which waited for: 6 -> 7; matrix products, arithmetic and copies ran while one was open for 6% -> 8% of each run, Pallas kernels for 0% -> 0%
where the time goes in v6:
time: 198 us; the launch traced here: 197 us
  waiting for transfers between devices  93.1 us (47%)
  blocking collectives  27.8 us (14%)
  starting transfers between devices  25.3 us (13%)
  between operations  13.7 us (7%)
  local copies, waits for them, and re-layouts  13.4 us (7%)
  matrix products  12.1 us (6%)
  other arithmetic  11.8 us (6%)
    reduce_scatter x1, waiting for transfers between devices, per_device(): lax.psum_scatter(paired, ('zh', 'zl'), scatter_dimension=0, tiled=True)[0]  68 us
    all_gather x1, blocking collectives, gather_block(): high = lax.all_gather(rows_here, 'zh', axis=0, tiled=True)  27.8 us
    all_gather x1, waiting for transfers between devices, gather_block(): mine = lax.all_gather(high, 'zl', axis=0, tiled=True)  11.3 us
    all_to_all x1, starting transfers between devices, per_device(): lax.all_to_all(jnp.broadcast_to(stats[None], (owners, *stats.shape)), 'ce...  8.46 us
    all_to_all x1, starting transfers between devices, per_device(): lax.all_to_all(slot_routes, 'cent', split_axis=0, concat_axis=0, tiled=True)  7.42 us
    dot_general x2, matrix products, owner_sums(): lax.dot_general(picked, widened, (((0,), (0,)), ((), ())), preferred_elem...  6.42 us
    all_to_all x1, starting transfers between devices, per_device(): lax.all_to_all(outgoing, 'cent', split_axis=0, concat_axis=0, tiled=True)  5.58 us
    all_to_all x1, waiting for transfers between devices, per_device(): lax.all_to_all(jnp.broadcast_to(stats[None], (owners, *stats.shape)), 'ce...  5.42 us
  transfers between devices with their start and end apart: 7, of which 7 were waited for; matrix products, arithmetic and copies ran while one was open for 8% of the time, Pallas kernels for 0%

profile of v6, /device:TPU:6, one launch (start us, length us, event | category | flops | bytes accessed | tf_op | source)
XLA Modules:
  0.0 197.2 jit_solution(15246321003188597228)
XLA Ops:
  6.5 27.8 %all-gather = bf16[1,128,1024]{2,1,0:T(8,128)(2,1)} all-gather(bf16[1,32,1024]{2,1,0:T(8,128)(2,1)} %param.7), channel_id=2, replica_groups=mesh['zh'=4,'zl'=4,'core'=2,'cent'=16] {'zh'}, dimensions={1}, use_global_device_ids=true | all-gather | bytes 327680 | tf_op jit(solution)/shard_map/all_gather | solution.py:22
  39.2 7.4 %all-to-all-start.1 = ((s32[16,2,3]{2,1,0:T(2,128)}), s32[16,2,3]{2,1,0:T(2,128)S(1)}, u32[]{:S(2)}, u32[]{:S(2)}) async-start(s32[16,2,3]{2,1,0:T(2,128)} %bitcast.11), calls=%async_computation.1 | async-start | bytes 32768 | tf_op jit(solution)/shard_map/all_to_all | solution.py:66
  47.6 2.4 %reshape.130 = bf16[16,64,1024]{2,1,0:T(8,128)(2,1)} reshape(bf16[32,32768]{1,0:T(8,128)(2,1)S(1)} %convolution_convert_fusion) | data formatting | bytes 4194304 | tf_op jit(solution)/shard_map/reshape | solution.py:59
  50.0 2.3 %all-to-all-done.1 = s32[16,2,3]{2,1,0:T(2,128)S(1)} async-done(((s32[16,2,3]{2,1,0:T(2,128)}), s32[16,2,3]{2,1,0:T(2,128)S(1)}, u32[]{:S(2)}, u32[]{:S(2)}) %all-to-all-start.1) | async-done | bytes 416 | tf_op jit(solution)/shard_map/all_to_all | solution.py:66
  52.3 5.6 %all-to-all-start = ((bf16[16,64,1024]{2,1,0:T(8,128)(2,1)}), bf16[16,64,1024]{2,1,0:T(8,128)(2,1)S(1)}, u32[]{:S(2)}, u32[]{:S(2)}) async-start(bf16[16,64,1024]{2,1,0:T(8,128)(2,1)} %reshape.130), calls=%async_computation | async-start | bytes 4194304 | tf_op jit(solution)/shard_map/all_to_all | solution.py:65
  57.9 11.3 %all-gather.4.cloned.1.call-done = bf16[1,512,1024]{2,1,0:T(8,128)(2,1)} async-done(((bf16[1,128,1024]{2,1,0:T(8,128)(2,1)}), bf16[1,512,1024]{2,1,0:T(8,128)(2,1)}) %all-gather.4.cloned.1.call-update) | async-done | bytes 1048592 | tf_op jit(solution)/shard_map/all_gather | solution.py:23
  69.2 1.9 collective-permute-start
  71.9 2.1 %collective-permute-done = bf16[512,1024]{1,0:T(8,128)(2,1)S(1)} collective-permute-done((bf16[512,1024]{1,0:T(8,128)(2,1)}, bf16[512,1024]{1,0:T(8,128)(2,1)S(1)}, u32[]{:S(2)}, u32[]{:S(2)}) %collective-permute-start) | collective-permute-done | bytes 1048608 | tf_op jit(solution)/shard_map/ppermute | solution.py:24
  73.9 1.4 broadcast_select_fusion.1
  75.5 1.5 copy.66
  77.0 2.7 %all-to-all-done = bf16[16,64,1024]{2,1,0:T(8,128)(2,1)S(1)} async-done(((bf16[16,64,1024]{2,1,0:T(8,128)(2,1)}), bf16[16,64,1024]{2,1,0:T(8,128)(2,1)S(1)}, u32[]{:S(2)}, u32[]{:S(2)}) %all-to-all-start) | async-done | bytes 2097184 | tf_op jit(solution)/shard_map/all_to_all | solution.py:65
  79.7 4.7 %multiply_reduce_fusion = (f32[1024]{0:T(1024)S(1)}, f32[1024,1024]{0,1:T(8,128)S(1)}) fusion(bf16[1024,1024]{1,0:T(8,128)(2,1)S(1)} %bitcast.61, bf16[1024,1024]{1,0:T(8,128)(2,1)} %bitcast.64), kind=kOutput, calls=%fused_computation.6 | convolution fusion | flops 2149579776 | bytes 8392704 | tf_op jit(solution)/shard_map/dot_general | solution.py:69
  84.4 2.0 %copy-done = f32[1024,1024]{0,1:T(8,128)} copy-done((f32[1024,1024]{0,1:T(8,128)}, f32[1024,1024]{0,1:T(8,128)S(1)}, u32[]{:S(2)}) %copy-start) | copy-done | bytes 4194328
  87.9 8.5 %all-to-all-start.2 = ((f32[16,2,1024]{2,1,0:T(2,128)}), f32[16,2,1024]{2,1,0:T(2,128)S(1)}, u32[]{:S(2)}, u32[]{:S(2)}) async-start(f32[16,2,1024]{2,1,0:T(2,128)} %broadcast_in_dim.89), calls=%async_computation.2 | async-start | bytes 262144 | tf_op jit(solution)/shard_map/all_to_all | solution.py:80
  96.7 5.4 %all-to-all-done.2 = f32[16,2,1024]{2,1,0:T(2,128)S(1)} async-done(((f32[16,2,1024]{2,1,0:T(2,128)}), f32[16,2,1024]{2,1,0:T(2,128)S(1)}, u32[]{:S(2)}, u32[]{:S(2)}) %all-to-all-start.2) | async-done | bytes 131104 | tf_op jit(solution)/shard_map/all_to_all | solution.py:80
  102.6 1.2 gather_fusion.1
  105.6 2.8 %exponential_convert_fusion = bf16[1024,1024]{0,1:T(8,128)(2,1)S(1)} fusion(f32[1024,1024]{0,1:T(8,128)} %copy-done, f32[1024]{0:T(1024)S(1)} %select_n.87), kind=kLoop, calls=%fused_computation.4 | loop fusion | flops 3145728 | bytes 6295552 | tf_op jit(solution)/shard_map/convert_element_type | solution.py:97
  108.4 3.0 %fusion = f32[16,32,1152]{2,1,0:T(8,128)} fusion(bf16[1024,1024]{1,0:T(8,128)(2,1)S(1)} %bitcast.62, bf16[1152]{0:T(1024)(128)(2,1)S(1)} %pad.1.clone, bf16[1024,16,2,32]{0,3,2,1:T(8,128)(2,1)S(1)} %bitcast.65, s32[]{:T(128)S(6)} %select_n.89), kind=kOutput, calls=%fused_computation.9 | convolution fusion | flops 1212678144 | bytes 5509124 | tf_op jit(solution)/shard_map/dot_general | solution.py:110
  111.4 1.9 collective-permute-start.1
  113.3 3.5 %fusion.1 = f32[16,32,1152]{2,1,0:T(8,128)S(1)} fusion(bf16[1024,1024]{1,0:T(8,128)(2,1)} %bitcast.63, bf16[1152]{0:T(1024)(128)(2,1)S(1)} %pad.1.clone, bf16[1024,16,2,32]{0,3,2,1:T(8,128)(2,1)} %bitcast.66, s32[]{:T(128)S(6)} %select_n.88), kind=kOutput, calls=%fused_computation.10 | convolution fusion | flops 1212678144 | bytes 5507332 | tf_op jit(solution)/shard_map/dot_general | solution.py:110
  116.8 1.2 collective-permute-done.1
  118.0 1.7 add.69
  119.8 68.0 %reduce-scatter.2.cloned.1.call-done = f32[1,32,1152]{2,1,0:T(8,128)} async-done(((f32[16,32,1152]{2,1,0:T(8,128)}), f32[1,32,1152]{2,1,0:T(8,128)}) %reduce-scatter.2.cloned.1.call-update) | async-done | bytes 147472 | tf_op jit(solution)/shard_map/reduce_scatter | solution.py:116
  188.7 1.6 fusion.11
  (65 shorter events, 11.5 us)
Async XLA Ops:
  6.5 62.7 %all-gather.4.cloned.1.call-start = ((), (), s32[]{:S(2)}) async-start(), calls=%async_computation.5 | async-start | bytes 1310720 | tf_op jit(solution)/shard_map/all_gather | solution.py:23
  34.4 3.9 %copy-start.5 = (s32[8]{0:T(128)S(1)}, s32[8]{0:T(128)}, u32[]{:S(2)}) copy-start(s32[8]{0:T(128)} %param.6) | copy-start | bytes 100
  34.4 12.3 %copy-start.3 = (bf16[256,1024]{1,0:T(8,128)(2,1)S(1)}, bf16[256,1024]{1,0:T(8,128)(2,1)}, u32[]{:S(2)}) copy-start(bf16[256,1024]{1,0:T(8,128)(2,1)} %param.4) | copy-start | bytes 1572868
  39.2 13.0 %all-to-all-start.1 = ((s32[16,2,3]{2,1,0:T(2,128)}), s32[16,2,3]{2,1,0:T(2,128)S(1)}, u32[]{:S(2)}, u32[]{:S(2)}) async-start(s32[16,2,3]{2,1,0:T(2,128)} %bitcast.11), calls=%async_computation.1 | async-start | bytes 32768 | tf_op jit(solution)/shard_map/all_to_all | solution.py:66
  52.3 27.4 %all-to-all-start = ((bf16[16,64,1024]{2,1,0:T(8,128)(2,1)}), bf16[16,64,1024]{2,1,0:T(8,128)(2,1)S(1)}, u32[]{:S(2)}, u32[]{:S(2)}) async-start(bf16[16,64,1024]{2,1,0:T(8,128)(2,1)} %reshape.130), calls=%async_computation | async-start | bytes 4194304 | tf_op jit(solution)/shard_map/all_to_all | solution.py:65
  69.2 4.8 %collective-permute-start = (bf16[512,1024]{1,0:T(8,128)(2,1)}, bf16[512,1024]{1,0:T(8,128)(2,1)S(1)}, u32[]{:S(2)}, u32[]{:S(2)}) collective-permute-start(bf16[512,1024]{1,0:T(8,128)(2,1)} %bitcast.67), channel_id=1, source_target_pairs={{0,16},{16,0},{1,17},{17,1},{2,18},{18,2},{3,19},{19,3},{4,20},{20... | collective-permute-start | bytes 3145736 | tf_op jit(solution)/shard_map/ppermute | solution.py:24
  79.7 28.8 %copy-start.1 = (bf16[16,64,1024]{2,1,0:T(8,128)(2,1)}, bf16[16,64,1024]{2,1,0:T(8,128)(2,1)S(1)}, u32[]{:S(2)}) copy-start(bf16[16,64,1024]{2,1,0:T(8,128)(2,1)S(1)} %all-to-all-done) | copy-start | bytes 6291460
  84.4 2.0 %copy-start = (f32[1024,1024]{0,1:T(8,128)}, f32[1024,1024]{0,1:T(8,128)S(1)}, u32[]{:S(2)}) copy-start(f32[1024,1024]{0,1:T(8,128)S(1)} %get-tuple-element.16) | copy-start | bytes 12582916
  87.9 14.3 %all-to-all-start.2 = ((f32[16,2,1024]{2,1,0:T(2,128)}), f32[16,2,1024]{2,1,0:T(2,128)S(1)}, u32[]{:S(2)}, u32[]{:S(2)}) async-start(f32[16,2,1024]{2,1,0:T(2,128)} %broadcast_in_dim.89), calls=%async_computation.2 | async-start | bytes 262144 | tf_op jit(solution)/shard_map/all_to_all | solution.py:80
  96.3 91.5 %reduce-scatter.2.cloned.1.call-start = ((), (), s32[]{:S(2)}) async-start(), calls=%async_computation.4 | async-start | bytes 2506752 | tf_op jit(solution)/shard_map/reduce_scatter | solution.py:116
  108.4 3.0 %copy-start.2 = (bf16[1024,1024]{0,1:T(8,128)(2,1)}, bf16[1024,1024]{0,1:T(8,128)(2,1)S(1)}, u32[]{:S(2)}) copy-start(bf16[1024,1024]{0,1:T(8,128)(2,1)S(1)} %exponential_convert_fusion) | copy-start | bytes 6291460
  111.4 6.6 %collective-permute-start.1 = (f32[16,32,1152]{2,1,0:T(8,128)}, f32[16,32,1152]{2,1,0:T(8,128)S(1)}, u32[]{:S(2)}, u32[]{:S(2)}) collective-permute-start(f32[16,32,1152]{2,1,0:T(8,128)} %fusion), channel_id=1, source_target_pairs={{0,16},{16,0},{1,17},{17,1},{2,18},{18,2},{3,19},{19,3},{4,20},{20... | collective-permute-start | bytes 7077896 | tf_op jit(solution)/shard_map/ppermute | solution.py:114
  119.8 68.9 %copy-start.4 = (bf16[1,32,1024]{2,1,0:T(8,128)(2,1)S(1)}, bf16[1,32,1024]{2,1,0:T(8,128)(2,1)}, u32[]{:S(2)}) copy-start(bf16[1,32,1024]{2,1,0:T(8,128)(2,1)} %param.7) | copy-start | bytes 196612
Sparse Core Ops, SparseCore 0:
  34.5 34.6 all-gather.3
  119.9 67.8 reduce-scatter.1

commit v7 on v6

--- a/solution.py
+++ b/solution.py
@@ -19,7 +19,9 @@
 
 def gather_block(rows_here):
     core = lax.axis_index("core")
-    high = lax.all_gather(rows_here, "zh", axis=0, tiled=True)
+    spread = jnp.broadcast_to(rows_here[None], (lax.axis_size("zh"), *rows_here.shape))
+    high = lax.all_to_all(spread, "zh", split_axis=0, concat_axis=0, tiled=True)
+    high = high.reshape(-1, rows_here.shape[-1])
     mine = lax.all_gather(high, "zl", axis=0, tiled=True)
     other = lax.ppermute(mine, "core", [(0, 1), (1, 0)])
     first = jnp.where(core == 0, mine, other)

time: 198 us -> 205 us (1.035)
  blocking collectives: 27.8 us -> 0 us
  waiting for transfers between devices: 93.1 us -> 111 us
  starting transfers between devices: 25.3 us -> 39.2 us
  local copies, waits for them, and re-layouts: 13.4 us -> 15.6 us
    all_gather x1 -> x0, blocking collectives: 27.8 us -> none  [gather_block(): high = lax.all_gather(rows_here, 'zh', axis=0, tiled=True)]
    all_to_all x0 -> x1, waiting for transfers between devices: none -> 15.9 us  [gather_block(): high = lax.all_to_all(spread, 'zh', split_axis=0, concat_axis=0, tiled=True)]
    all_to_all x0 -> x1, starting transfers between devices: none -> 15.1 us  [gather_block(): high = lax.all_to_all(spread, 'zh', split_axis=0, concat_axis=0, tiled=True)]
    reduce_scatter x1, waiting for transfers between devices: 68 us -> 70.9 us  [per_device(): lax.psum_scatter(paired, ('zh', 'zl'), scatter_dimension=0, tiled=True)[0]]
    all_to_all x1, waiting for transfers between devices: 2.68 us -> 0.49 us  [per_device(): lax.all_to_all(outgoing, 'cent', split_axis=0, concat_axis=0, tiled=True)]
  transfers between devices with their start and end apart: 7 -> 8, of which waited for: 7 -> 8; matrix products, arithmetic and copies ran while one was open for 8% -> 8% of each run, Pallas kernels for 0% -> 0%
where the time goes in v7:
time: 205 us; the launch traced here: 204 us
  waiting for transfers between devices  111 us (54%)
  starting transfers between devices  39.2 us (19%)
  local copies, waits for them, and re-layouts  15.6 us (8%)
  between operations  13.6 us (7%)
  matrix products  12.1 us (6%)
  other arithmetic  11.8 us (6%)
    reduce_scatter x1, waiting for transfers between devices, per_device(): lax.psum_scatter(paired, ('zh', 'zl'), scatter_dimension=0, tiled=True)[0]  70.9 us
    all_to_all x1, waiting for transfers between devices, gather_block(): high = lax.all_to_all(spread, 'zh', split_axis=0, concat_axis=0, tiled=True)  15.9 us
    all_to_all x1, starting transfers between devices, gather_block(): high = lax.all_to_all(spread, 'zh', split_axis=0, concat_axis=0, tiled=True)  15.1 us
    all_gather x1, waiting for transfers between devices, gather_block(): mine = lax.all_gather(high, 'zl', axis=0, tiled=True)  13 us
    all_to_all x1, starting transfers between devices, per_device(): lax.all_to_all(slot_routes, 'cent', split_axis=0, concat_axis=0, tiled=True)  7.42 us
    all_to_all x1, starting transfers between devices, per_device(): lax.all_to_all(jnp.broadcast_to(stats[None], (owners, *stats.shape)), 'ce...  7.22 us
    dot_general x2, matrix products, owner_sums(): lax.dot_general(picked, widened, (((0,), (0,)), ((), ())), preferred_elem...  6.43 us
    all_to_all x1, starting transfers between devices, per_device(): lax.all_to_all(outgoing, 'cent', split_axis=0, concat_axis=0, tiled=True)  5.58 us
  transfers between devices with their start and end apart: 8, of which 8 were waited for; matrix products, arithmetic and copies ran while one was open for 8% of the time, Pallas kernels for 0%

profile of v7, /device:TPU:6, one launch (start us, length us, event | category | flops | bytes accessed | tf_op | source)
XLA Modules:
  0.0 203.6 jit_solution(3317106656340210909)
XLA Ops:
  6.5 1.6 broadcast_in_dim.94
  8.1 15.1 %all-to-all-start.1 = ((bf16[4,32,1024]{2,1,0:T(8,128)(2,1)}), bf16[4,32,1024]{2,1,0:T(8,128)(2,1)S(1)}, u32[]{:S(2)}, u32[]{:S(2)}) async-start(bf16[4,32,1024]{2,1,0:T(8,128)(2,1)} %broadcast_in_dim.94), calls=%async_computation.1 | async-start | bytes 524288 | tf_op jit(solution)/shard_map/all_to_all | solution.py:23
  25.9 15.9 %all-to-all-done.1 = bf16[4,32,1024]{2,1,0:T(8,128)(2,1)S(1)} async-done(((bf16[4,32,1024]{2,1,0:T(8,128)(2,1)}), bf16[4,32,1024]{2,1,0:T(8,128)(2,1)S(1)}, u32[]{:S(2)}, u32[]{:S(2)}) %all-to-all-start.1) | async-done | bytes 262176 | tf_op jit(solution)/shard_map/all_to_all | solution.py:23
  44.6 7.4 %all-to-all-start.2 = ((s32[16,2,3]{2,1,0:T(2,128)}), s32[16,2,3]{2,1,0:T(2,128)S(1)}, u32[]{:S(2)}, u32[]{:S(2)}) async-start(s32[16,2,3]{2,1,0:T(2,128)} %bitcast.12), calls=%async_computation.2 | async-start | bytes 32768 | tf_op jit(solution)/shard_map/all_to_all | solution.py:68
  53.0 2.4 %reshape.133 = bf16[16,64,1024]{2,1,0:T(8,128)(2,1)} reshape(bf16[32,32768]{1,0:T(8,128)(2,1)S(1)} %convolution_convert_fusion) | data formatting | bytes 4194304 | tf_op jit(solution)/shard_map/reshape | solution.py:61
  55.4 2.3 %all-to-all-done.2 = s32[16,2,3]{2,1,0:T(2,128)S(1)} async-done(((s32[16,2,3]{2,1,0:T(2,128)}), s32[16,2,3]{2,1,0:T(2,128)S(1)}, u32[]{:S(2)}, u32[]{:S(2)}) %all-to-all-start.2) | async-done | bytes 416 | tf_op jit(solution)/shard_map/all_to_all | solution.py:68
  57.7 5.6 %all-to-all-start = ((bf16[16,64,1024]{2,1,0:T(8,128)(2,1)}), bf16[16,64,1024]{2,1,0:T(8,128)(2,1)S(1)}, u32[]{:S(2)}, u32[]{:S(2)}) async-start(bf16[16,64,1024]{2,1,0:T(8,128)(2,1)} %reshape.133), calls=%async_computation | async-start | bytes 4194304 | tf_op jit(solution)/shard_map/all_to_all | solution.py:67
  63.2 13.0 %all-gather.2.cloned.1.call-done = bf16[512,1024]{1,0:T(8,128)(2,1)} async-done(((bf16[128,1024]{1,0:T(8,128)(2,1)}), bf16[512,1024]{1,0:T(8,128)(2,1)}) %all-gather.2.cloned.1.call-update) | async-done | bytes 1048592 | tf_op jit(solution)/shard_map/all_gather | solution.py:25
  76.2 1.9 collective-permute-start
  78.9 2.1 %collective-permute-done = bf16[512,1024]{1,0:T(8,128)(2,1)S(1)} collective-permute-done((bf16[512,1024]{1,0:T(8,128)(2,1)}, bf16[512,1024]{1,0:T(8,128)(2,1)S(1)}, u32[]{:S(2)}, u32[]{:S(2)}) %collective-permute-start) | collective-permute-done | bytes 1048608 | tf_op jit(solution)/shard_map/ppermute | solution.py:26
  81.0 1.4 broadcast_select_fusion.1
  82.5 1.5 copy.66
  84.5 4.7 %multiply_reduce_fusion = (f32[1024]{0:T(1024)S(1)}, f32[1024,1024]{0,1:T(8,128)S(1)}) fusion(bf16[1024,1024]{1,0:T(8,128)(2,1)S(1)} %bitcast.58, bf16[1024,1024]{1,0:T(8,128)(2,1)} %bitcast.61), kind=kOutput, calls=%fused_computation.6 | convolution fusion | flops 2149579776 | bytes 8392704 | tf_op jit(solution)/shard_map/dot_general | solution.py:71
  89.2 2.0 copy-done
  92.7 7.2 %all-to-all-start.3 = ((f32[16,2,1024]{2,1,0:T(2,128)}), f32[16,2,1024]{2,1,0:T(2,128)S(1)}, u32[]{:S(2)}, u32[]{:S(2)}) async-start(f32[16,2,1024]{2,1,0:T(2,128)} %broadcast_in_dim.98), calls=%async_computation.3 | async-start | bytes 262144 | tf_op jit(solution)/shard_map/all_to_all | solution.py:82
  100.3 5.4 %all-to-all-done.3 = f32[16,2,1024]{2,1,0:T(2,128)S(1)} async-done(((f32[16,2,1024]{2,1,0:T(2,128)}), f32[16,2,1024]{2,1,0:T(2,128)S(1)}, u32[]{:S(2)}, u32[]{:S(2)}) %all-to-all-start.3) | async-done | bytes 131104 | tf_op jit(solution)/shard_map/all_to_all | solution.py:82
  109.1 2.8 %exponential_convert_fusion = bf16[1024,1024]{0,1:T(8,128)(2,1)S(1)} fusion(f32[1024,1024]{0,1:T(8,128)} %copy-done, f32[1024]{0:T(1024)S(1)} %select_n.87), kind=kLoop, calls=%fused_computation.4 | loop fusion | flops 3145728 | bytes 6295552 | tf_op jit(solution)/shard_map/convert_element_type | solution.py:99
  112.0 3.0 %fusion = f32[16,32,1152]{2,1,0:T(8,128)} fusion(bf16[1024,1024]{1,0:T(8,128)(2,1)S(1)} %bitcast.59, bf16[1152]{0:T(1024)(128)(2,1)S(1)} %pad.1.clone, bf16[1024,16,2,32]{0,3,2,1:T(8,128)(2,1)S(1)} %bitcast.62, s32[]{:T(128)S(6)} %select_n.89), kind=kOutput, calls=%fused_computation.9 | convolution fusion | flops 1212678144 | bytes 5509124 | tf_op jit(solution)/shard_map/dot_general | solution.py:112
  115.0 1.9 collective-permute-start.1
  116.9 3.5 %fusion.1 = f32[16,32,1152]{2,1,0:T(8,128)S(1)} fusion(bf16[1024,1024]{1,0:T(8,128)(2,1)} %bitcast.60, bf16[1152]{0:T(1024)(128)(2,1)S(1)} %pad.1.clone, bf16[1024,16,2,32]{0,3,2,1:T(8,128)(2,1)} %bitcast.63, s32[]{:T(128)S(6)} %select_n.88), kind=kOutput, calls=%fused_computation.10 | convolution fusion | flops 1212678144 | bytes 5507332 | tf_op jit(solution)/shard_map/dot_general | solution.py:112
  120.3 1.2 collective-permute-done.1
  121.6 1.7 add.69
  123.4 70.9 %reduce-scatter.2.cloned.1.call-done = f32[1,32,1152]{2,1,0:T(8,128)} async-done(((f32[16,32,1152]{2,1,0:T(8,128)}), f32[1,32,1152]{2,1,0:T(8,128)}) %reduce-scatter.2.cloned.1.call-update) | async-done | bytes 147472 | tf_op jit(solution)/shard_map/reduce_scatter | solution.py:118
  195.1 1.6 fusion.11
  (69 shorter events, 13.9 us)
Async XLA Ops:
  8.1 33.6 %all-to-all-start.1 = ((bf16[4,32,1024]{2,1,0:T(8,128)(2,1)}), bf16[4,32,1024]{2,1,0:T(8,128)(2,1)S(1)}, u32[]{:S(2)}, u32[]{:S(2)}) async-start(bf16[4,32,1024]{2,1,0:T(8,128)(2,1)} %broadcast_in_dim.94), calls=%async_computation.1 | async-start | bytes 524288 | tf_op jit(solution)/shard_map/all_to_all | solution.py:23
  23.2 20.5 %copy-start.6 = (s32[8]{0:T(128)S(1)}, s32[8]{0:T(128)}, u32[]{:S(2)}) copy-start(s32[8]{0:T(128)} %param.6) | copy-start | bytes 100
  23.2 53.0 %all-gather.2.cloned.1.call-start = ((), (), s32[]{:S(2)}) async-start(), calls=%async_computation.5 | async-start | bytes 1310720 | tf_op jit(solution)/shard_map/all_gather | solution.py:25
  41.7 0.7 copy-start.3
  41.7 10.3 %copy-start.4 = (bf16[256,1024]{1,0:T(8,128)(2,1)S(1)}, bf16[256,1024]{1,0:T(8,128)(2,1)}, u32[]{:S(2)}) copy-start(bf16[256,1024]{1,0:T(8,128)(2,1)} %param.4) | copy-start | bytes 1572868
  44.6 13.0 %all-to-all-start.2 = ((s32[16,2,3]{2,1,0:T(2,128)}), s32[16,2,3]{2,1,0:T(2,128)S(1)}, u32[]{:S(2)}, u32[]{:S(2)}) async-start(s32[16,2,3]{2,1,0:T(2,128)} %bitcast.12), calls=%async_computation.2 | async-start | bytes 32768 | tf_op jit(solution)/shard_map/all_to_all | solution.py:68
  57.7 26.8 %all-to-all-start = ((bf16[16,64,1024]{2,1,0:T(8,128)(2,1)}), bf16[16,64,1024]{2,1,0:T(8,128)(2,1)S(1)}, u32[]{:S(2)}, u32[]{:S(2)}) async-start(bf16[16,64,1024]{2,1,0:T(8,128)(2,1)} %reshape.133), calls=%async_computation | async-start | bytes 4194304 | tf_op jit(solution)/shard_map/all_to_all | solution.py:67
  76.2 4.8 %collective-permute-start = (bf16[512,1024]{1,0:T(8,128)(2,1)}, bf16[512,1024]{1,0:T(8,128)(2,1)S(1)}, u32[]{:S(2)}, u32[]{:S(2)}) collective-permute-start(bf16[512,1024]{1,0:T(8,128)(2,1)} %all-gather.2.cloned.1.call-done), channel_id=1, source_target_pairs={{0,16},{16,0},{1,17},{17,1},{2,18},{18,2},{3,19},{19,3},{4,20},{20... | collective-permute-start | bytes 3145736 | tf_op jit(solution)/shard_map/ppermute | solution.py:26
  84.5 27.5 %copy-start.1 = (bf16[16,64,1024]{2,1,0:T(8,128)(2,1)}, bf16[16,64,1024]{2,1,0:T(8,128)(2,1)S(1)}, u32[]{:S(2)}) copy-start(bf16[16,64,1024]{2,1,0:T(8,128)(2,1)S(1)} %all-to-all-done) | copy-start | bytes 6291460
  89.2 2.0 copy-start
  92.7 13.0 %all-to-all-start.3 = ((f32[16,2,1024]{2,1,0:T(2,128)}), f32[16,2,1024]{2,1,0:T(2,128)S(1)}, u32[]{:S(2)}, u32[]{:S(2)}) async-start(f32[16,2,1024]{2,1,0:T(2,128)} %broadcast_in_dim.98), calls=%async_computation.3 | async-start | bytes 262144 | tf_op jit(solution)/shard_map/all_to_all | solution.py:82
  99.9 94.4 %reduce-scatter.2.cloned.1.call-start = ((), (), s32[]{:S(2)}) async-start(), calls=%async_computation.6 | async-start | bytes 2506752 | tf_op jit(solution)/shard_map/reduce_scatter | solution.py:118
  112.0 3.0 %copy-start.2 = (bf16[1024,1024]{0,1:T(8,128)(2,1)}, bf16[1024,1024]{0,1:T(8,128)(2,1)S(1)}, u32[]{:S(2)}) copy-start(bf16[1024,1024]{0,1:T(8,128)(2,1)S(1)} %exponential_convert_fusion) | copy-start | bytes 6291460
  115.0 6.6 %collective-permute-start.1 = (f32[16,32,1152]{2,1,0:T(8,128)}, f32[16,32,1152]{2,1,0:T(8,128)S(1)}, u32[]{:S(2)}, u32[]{:S(2)}) collective-permute-start(f32[16,32,1152]{2,1,0:T(8,128)} %fusion), channel_id=1, source_target_pairs={{0,16},{16,0},{1,17},{17,1},{2,18},{18,2},{3,19},{19,3},{4,20},{20... | collective-permute-start | bytes 7077896 | tf_op jit(solution)/shard_map/ppermute | solution.py:116
  123.3 71.8 %copy-start.5 = (bf16[1,32,1024]{2,1,0:T(8,128)(2,1)S(1)}, bf16[1,32,1024]{2,1,0:T(8,128)(2,1)}, u32[]{:S(2)}) copy-start(bf16[1,32,1024]{2,1,0:T(8,128)(2,1)} %param.7) | copy-start | bytes 196612
Sparse Core Ops, SparseCore 0:
  42.6 33.5 all-gather.1
  123.5 70.7 reduce-scatter.1

commit v8 on v6

--- a/solution.py
+++ b/solution.py
@@ -88,11 +88,8 @@
     held = arrived_routes >= 0
     code = jnp.maximum(arrived_routes, 0)
     source = jnp.arange(owners, dtype=jnp.int32)[:, None, None]
-    slot_norms = combine_norms(
-        every[code // capacity, 0, source, code % capacity],
-        every[code // capacity, 1, source, code % capacity],
-        held,
-    )
+    picked = every[code // capacity, :, source, code % capacity]
+    slot_norms = combine_norms(picked[..., 0, :], picked[..., 1, :], held)
     row_norms = jnp.where(jnp.any(held, axis=-1)[..., None], slot_norms, empty_norm).reshape(-1)
     shares = jnp.exp(logits - row_norms[:, None]).astype(jnp.bfloat16)
     own_rows = centroids[0].astype(jnp.float32)

time: 198 us -> 197 us (level)
  no operation moved by 1% of the time
where the time goes in v8:
time: 197 us
  waiting for transfers between devices  93.2 us (47%)
  blocking collectives  27.8 us (14%)
  starting transfers between devices  25.3 us (13%)
  between operations  13.6 us (7%)
  local copies, waits for them, and re-layouts  12.9 us (7%)
  matrix products  12.1 us (6%)
  other arithmetic  11.7 us (6%)
    reduce_scatter x1, waiting for transfers between devices, per_device(): lax.psum_scatter(paired, ('zh', 'zl'), scatter_dimension=0, tiled=True)[0]  68.1 us
    all_gather x1, blocking collectives, gather_block(): high = lax.all_gather(rows_here, 'zh', axis=0, tiled=True)  27.8 us
    all_gather x1, waiting for transfers between devices, gather_block(): mine = lax.all_gather(high, 'zl', axis=0, tiled=True)  11.3 us
    all_to_all x1, starting transfers between devices, per_device(): lax.all_to_all(jnp.broadcast_to(stats[None], (owners, *stats.shape)), 'ce...  8.46 us
    all_to_all x1, starting transfers between devices, per_device(): lax.all_to_all(slot_routes, 'cent', split_axis=0, concat_axis=0, tiled=True)  7.42 us
    dot_general x2, matrix products, owner_sums(): lax.dot_general(picked, widened, (((0,), (0,)), ((), ())), preferred_elem...  6.42 us
    all_to_all x1, starting transfers between devices, per_device(): lax.all_to_all(outgoing, 'cent', split_axis=0, concat_axis=0, tiled=True)  5.58 us
    all_to_all x1, waiting for transfers between devices, per_device(): lax.all_to_all(jnp.broadcast_to(stats[None], (owners, *stats.shape)), 'ce...  5.55 us
  transfers between devices with their start and end apart: 7, of which 7 were waited for; matrix products, arithmetic and copies ran while one was open for 8% of the time, Pallas kernels for 0%

profile of v8, /device:TPU:6, one launch (start us, length us, event | category | flops | bytes accessed | tf_op | source)
XLA Modules:
  0.0 196.6 jit_solution(16741518325068134499)
XLA Ops:
  6.5 27.8 %all-gather = bf16[1,128,1024]{2,1,0:T(8,128)(2,1)} all-gather(bf16[1,32,1024]{2,1,0:T(8,128)(2,1)} %param.7), channel_id=2, replica_groups=mesh['zh'=4,'zl'=4,'core'=2,'cent'=16] {'zh'}, dimensions={1}, use_global_device_ids=true | all-gather | bytes 327680 | tf_op jit(solution)/shard_map/all_gather | solution.py:22
  39.2 7.4 %all-to-all-start.1 = ((s32[16,2,3]{2,1,0:T(2,128)}), s32[16,2,3]{2,1,0:T(2,128)S(1)}, u32[]{:S(2)}, u32[]{:S(2)}) async-start(s32[16,2,3]{2,1,0:T(2,128)} %bitcast.11), calls=%async_computation.1 | async-start | bytes 32768 | tf_op jit(solution)/shard_map/all_to_all | solution.py:66
  47.6 2.4 %reshape.130 = bf16[16,64,1024]{2,1,0:T(8,128)(2,1)} reshape(bf16[32,32768]{1,0:T(8,128)(2,1)S(1)} %convolution_convert_fusion) | data formatting | bytes 4194304 | tf_op jit(solution)/shard_map/reshape | solution.py:59
  50.0 2.3 %all-to-all-done.1 = s32[16,2,3]{2,1,0:T(2,128)S(1)} async-done(((s32[16,2,3]{2,1,0:T(2,128)}), s32[16,2,3]{2,1,0:T(2,128)S(1)}, u32[]{:S(2)}, u32[]{:S(2)}) %all-to-all-start.1) | async-done | bytes 416 | tf_op jit(solution)/shard_map/all_to_all | solution.py:66
  52.3 5.6 %all-to-all-start = ((bf16[16,64,1024]{2,1,0:T(8,128)(2,1)}), bf16[16,64,1024]{2,1,0:T(8,128)(2,1)S(1)}, u32[]{:S(2)}, u32[]{:S(2)}) async-start(bf16[16,64,1024]{2,1,0:T(8,128)(2,1)} %reshape.130), calls=%async_computation | async-start | bytes 4194304 | tf_op jit(solution)/shard_map/all_to_all | solution.py:65
  57.9 11.3 %all-gather.4.cloned.1.call-done = bf16[1,512,1024]{2,1,0:T(8,128)(2,1)} async-done(((bf16[1,128,1024]{2,1,0:T(8,128)(2,1)}), bf16[1,512,1024]{2,1,0:T(8,128)(2,1)}) %all-gather.4.cloned.1.call-update) | async-done | bytes 1048592 | tf_op jit(solution)/shard_map/all_gather | solution.py:23
  69.2 1.9 collective-permute-start
  72.0 2.0 collective-permute-done
  73.9 1.4 broadcast_select_fusion.1
  75.5 1.5 copy.129
  77.0 2.7 %all-to-all-done = bf16[16,64,1024]{2,1,0:T(8,128)(2,1)S(1)} async-done(((bf16[16,64,1024]{2,1,0:T(8,128)(2,1)}), bf16[16,64,1024]{2,1,0:T(8,128)(2,1)S(1)}, u32[]{:S(2)}, u32[]{:S(2)}) %all-to-all-start) | async-done | bytes 2097184 | tf_op jit(solution)/shard_map/all_to_all | solution.py:65
  79.7 4.7 %multiply_reduce_fusion = (f32[1024]{0:T(1024)S(1)}, f32[1024,1024]{0,1:T(8,128)S(1)}) fusion(bf16[1024,1024]{1,0:T(8,128)(2,1)S(1)} %bitcast.69, bf16[1024,1024]{1,0:T(8,128)(2,1)} %bitcast.72), kind=kOutput, calls=%fused_computation.5 | convolution fusion | flops 2149579776 | bytes 8392704 | tf_op jit(solution)/shard_map/dot_general | solution.py:69
  84.4 2.0 %copy-done = f32[1024,1024]{0,1:T(8,128)} copy-done((f32[1024,1024]{0,1:T(8,128)}, f32[1024,1024]{0,1:T(8,128)S(1)}, u32[]{:S(2)}) %copy-start) | copy-done | bytes 4194328
  87.9 8.5 %all-to-all-start.2 = ((f32[16,2,1024]{2,1,0:T(2,128)}), f32[16,2,1024]{2,1,0:T(2,128)S(1)}, u32[]{:S(2)}, u32[]{:S(2)}) async-start(f32[16,2,1024]{2,1,0:T(2,128)} %broadcast_in_dim.76), calls=%async_computation.2 | async-start | bytes 262144 | tf_op jit(solution)/shard_map/all_to_all | solution.py:80
  96.6 5.6 %all-to-all-done.2 = f32[16,2,1024]{2,1,0:T(2,128)S(1)} async-done(((f32[16,2,1024]{2,1,0:T(2,128)}), f32[16,2,1024]{2,1,0:T(2,128)S(1)}, u32[]{:S(2)}, u32[]{:S(2)}) %all-to-all-start.2) | async-done | bytes 131104 | tf_op jit(solution)/shard_map/all_to_all | solution.py:80
  103.0 1.5 gather_fusion
  104.9 2.8 %exponential_convert_fusion = bf16[1024,1024]{0,1:T(8,128)(2,1)S(1)} fusion(f32[1024,1024]{0,1:T(8,128)} %copy-done, f32[1024]{0:T(1024)S(1)} %select_n.81), kind=kLoop, calls=%fused_computation.3 | loop fusion | flops 3145728 | bytes 6295552 | tf_op jit(solution)/shard_map/convert_element_type | solution.py:94
  107.8 3.0 %fusion = f32[16,32,1152]{2,1,0:T(8,128)} fusion(bf16[1024,1024]{1,0:T(8,128)(2,1)S(1)} %bitcast.70, bf16[1152]{0:T(1024)(128)(2,1)S(1)} %pad.1.clone, bf16[1024,16,2,32]{0,3,2,1:T(8,128)(2,1)S(1)} %bitcast.73, s32[]{:T(128)S(6)} %select_n.83), kind=kOutput, calls=%fused_computation.8 | convolution fusion | flops 1212678144 | bytes 5509124 | tf_op jit(solution)/shard_map/dot_general | solution.py:107
  110.8 1.9 collective-permute-start.1
  112.7 3.5 %fusion.1 = f32[16,32,1152]{2,1,0:T(8,128)S(1)} fusion(bf16[1024,1024]{1,0:T(8,128)(2,1)} %bitcast.71, bf16[1152]{0:T(1024)(128)(2,1)S(1)} %pad.1.clone, bf16[1024,16,2,32]{0,3,2,1:T(8,128)(2,1)} %bitcast.74, s32[]{:T(128)S(6)} %select_n.82), kind=kOutput, calls=%fused_computation.9 | convolution fusion | flops 1212678144 | bytes 5507332 | tf_op jit(solution)/shard_map/dot_general | solution.py:107
  116.2 1.2 collective-permute-done.1
  117.4 1.7 add.69
  119.2 68.1 %reduce-scatter.2.cloned.1.call-done = f32[1,32,1152]{2,1,0:T(8,128)} async-done(((f32[16,32,1152]{2,1,0:T(8,128)}), f32[1,32,1152]{2,1,0:T(8,128)}) %reduce-scatter.2.cloned.1.call-update) | async-done | bytes 147472 | tf_op jit(solution)/shard_map/reduce_scatter | solution.py:113
  188.1 1.6 fusion.11
  (65 shorter events, 10.6 us)
Async XLA Ops:
  6.5 62.7 %all-gather.4.cloned.1.call-start = ((), (), s32[]{:S(2)}) async-start(), calls=%async_computation.5 | async-start | bytes 1310720 | tf_op jit(solution)/shard_map/all_gather | solution.py:23
  34.4 3.9 %copy-start.5 = (s32[8]{0:T(128)S(1)}, s32[8]{0:T(128)}, u32[]{:S(2)}) copy-start(s32[8]{0:T(128)} %param.6) | copy-start | bytes 100
  34.4 12.3 %copy-start.3 = (bf16[256,1024]{1,0:T(8,128)(2,1)S(1)}, bf16[256,1024]{1,0:T(8,128)(2,1)}, u32[]{:S(2)}) copy-start(bf16[256,1024]{1,0:T(8,128)(2,1)} %param.4) | copy-start | bytes 1572868
  39.2 13.0 %all-to-all-start.1 = ((s32[16,2,3]{2,1,0:T(2,128)}), s32[16,2,3]{2,1,0:T(2,128)S(1)}, u32[]{:S(2)}, u32[]{:S(2)}) async-start(s32[16,2,3]{2,1,0:T(2,128)} %bitcast.11), calls=%async_computation.1 | async-start | bytes 32768 | tf_op jit(solution)/shard_map/all_to_all | solution.py:66
  52.3 27.4 %all-to-all-start = ((bf16[16,64,1024]{2,1,0:T(8,128)(2,1)}), bf16[16,64,1024]{2,1,0:T(8,128)(2,1)S(1)}, u32[]{:S(2)}, u32[]{:S(2)}) async-start(bf16[16,64,1024]{2,1,0:T(8,128)(2,1)} %reshape.130), calls=%async_computation | async-start | bytes 4194304 | tf_op jit(solution)/shard_map/all_to_all | solution.py:65
  69.2 4.8 %collective-permute-start = (bf16[512,1024]{1,0:T(8,128)(2,1)}, bf16[512,1024]{1,0:T(8,128)(2,1)S(1)}, u32[]{:S(2)}, u32[]{:S(2)}) collective-permute-start(bf16[512,1024]{1,0:T(8,128)(2,1)} %bitcast.75), channel_id=1, source_target_pairs={{0,16},{16,0},{1,17},{17,1},{2,18},{18,2},{3,19},{19,3},{4,20},{20... | collective-permute-start | bytes 3145736 | tf_op jit(solution)/shard_map/ppermute | solution.py:24
  79.7 28.1 %copy-start.1 = (bf16[16,64,1024]{2,1,0:T(8,128)(2,1)}, bf16[16,64,1024]{2,1,0:T(8,128)(2,1)S(1)}, u32[]{:S(2)}) copy-start(bf16[16,64,1024]{2,1,0:T(8,128)(2,1)S(1)} %all-to-all-done) | copy-start | bytes 6291460
  84.4 2.0 %copy-start = (f32[1024,1024]{0,1:T(8,128)}, f32[1024,1024]{0,1:T(8,128)S(1)}, u32[]{:S(2)}) copy-start(f32[1024,1024]{0,1:T(8,128)S(1)} %get-tuple-element.16) | copy-start | bytes 12582916
  87.9 14.3 %all-to-all-start.2 = ((f32[16,2,1024]{2,1,0:T(2,128)}), f32[16,2,1024]{2,1,0:T(2,128)S(1)}, u32[]{:S(2)}, u32[]{:S(2)}) async-start(f32[16,2,1024]{2,1,0:T(2,128)} %broadcast_in_dim.76), calls=%async_computation.2 | async-start | bytes 262144 | tf_op jit(solution)/shard_map/all_to_all | solution.py:80
  96.3 90.9 %reduce-scatter.2.cloned.1.call-start = ((), (), s32[]{:S(2)}) async-start(), calls=%async_computation.4 | async-start | bytes 2506752 | tf_op jit(solution)/shard_map/reduce_scatter | solution.py:113
  107.8 3.0 %copy-start.2 = (bf16[1024,1024]{0,1:T(8,128)(2,1)}, bf16[1024,1024]{0,1:T(8,128)(2,1)S(1)}, u32[]{:S(2)}) copy-start(bf16[1024,1024]{0,1:T(8,128)(2,1)S(1)} %exponential_convert_fusion) | copy-start | bytes 6291460
  110.8 6.6 %collective-permute-start.1 = (f32[16,32,1152]{2,1,0:T(8,128)}, f32[16,32,1152]{2,1,0:T(8,128)S(1)}, u32[]{:S(2)}, u32[]{:S(2)}) collective-permute-start(f32[16,32,1152]{2,1,0:T(8,128)} %fusion), channel_id=1, source_target_pairs={{0,16},{16,0},{1,17},{17,1},{2,18},{18,2},{3,19},{19,3},{4,20},{20... | collective-permute-start | bytes 7077896 | tf_op jit(solution)/shard_map/ppermute | solution.py:111
  119.1 69.0 %copy-start.4 = (bf16[1,32,1024]{2,1,0:T(8,128)(2,1)S(1)}, bf16[1,32,1024]{2,1,0:T(8,128)(2,1)}, u32[]{:S(2)}) copy-start(bf16[1,32,1024]{2,1,0:T(8,128)(2,1)} %param.7) | copy-start | bytes 196612
Sparse Core Ops, SparseCore 0:
  34.5 34.6 all-gather.3
  119.3 67.9 reduce-scatter.1

commit v9 on v8

--- a/solution.py
+++ b/solution.py
@@ -18,15 +18,10 @@
 
 
 def gather_block(rows_here):
-    core = lax.axis_index("core")
     high = lax.all_gather(rows_here, "zh", axis=0, tiled=True)
     mine = lax.all_gather(high, "zl", axis=0, tiled=True)
     other = lax.ppermute(mine, "core", [(0, 1), (1, 0)])
-    first = jnp.where(core == 0, mine, other)
-    second = jnp.where(core == 0, other, mine)
-    shape = (lax.axis_size("zl"), lax.axis_size("zh"), *rows_here.shape)
-    both = jnp.stack([first.reshape(shape), second.reshape(shape)], axis=2)
-    return both.transpose(1, 0, 2, 3, 4).reshape(-1, rows_here.shape[-1])
+    return jnp.concatenate([mine, other], axis=0)
 
 
 def per_device(points, block_list, list_count, centroids):
@@ -97,19 +92,18 @@
     widened = jnp.concatenate(
         [incoming, jnp.broadcast_to(marker[None, :], (incoming.shape[0], 128))], axis=1
     )
-    n_core = lax.axis_size("core")
-    core = lax.axis_index("core")
-    n_z = lax.axis_size("zh") * lax.axis_size("zl")
-    by_owner = shares.reshape(shares.shape[0], n_z, n_core, -1)
+    n_high, n_low = lax.axis_size("zh"), lax.axis_size("zl")
+    halves = shares.reshape(shares.shape[0], 2, -1)
 
-    def owner_sums(which):
-        picked = lax.dynamic_index_in_dim(by_owner, which, axis=2, keepdims=False)
+    def half_sums(which):
         return lax.dot_general(
-            picked, widened, (((0,), (0,)), ((), ())), preferred_element_type=jnp.float32
+            halves[:, which], widened, (((0,), (0,)), ((), ())), preferred_element_type=jnp.float32
         )
 
-    sent = lax.ppermute(owner_sums(n_core - 1 - core), "core", [(0, 1), (1, 0)])
-    paired = lax.optimization_barrier(owner_sums(core)) + sent
+    sent = lax.ppermute(half_sums(1), "core", [(0, 1), (1, 0)])
+    paired = lax.optimization_barrier(half_sums(0)) + sent
+    paired = paired.reshape(n_low, n_high, -1, paired.shape[-1]).transpose(1, 0, 2, 3)
+    paired = paired.reshape(n_high * n_low, -1, paired.shape[-1])
     reduced = lax.psum_scatter(paired, ("zh", "zl"), scatter_dimension=0, tiled=True)[0]
     new_sums = reduced[:, :width]
     new_mass = reduced[:, width]

time: 197 us -> 195 us (0.990)
  waiting for transfers between devices: 93.2 us -> 97.9 us
  matrix products: 12.1 us -> 7.94 us
  other arithmetic: 11.7 us -> 8.59 us
    all_to_all x1, waiting for transfers between devices: 2.68 us -> 7.69 us  [per_device(): lax.all_to_all(outgoing, 'cent', split_axis=0, concat_axis=0, tiled=True)]
    dot_general x2, matrix products: 6.42 us -> 3.09 us  [half_sums(): lax.dot_general(halves[:, which], widened, (((0,), (0,)), ((), ())), pref...]
  transfers between devices with their start and end apart: 7 -> 7, of which waited for: 7 -> 6; matrix products, arithmetic and copies ran while one was open for 8% -> 6% of each run, Pallas kernels for 0% -> 0%
where the time goes in v9:
time: 195 us; the launch traced here: 194 us
  waiting for transfers between devices  97.9 us (50%)
  blocking collectives  27.8 us (14%)
  starting transfers between devices  25.3 us (13%)
  between operations  13.6 us (7%)
  local copies, waits for them, and re-layouts  12.9 us (7%)
  other arithmetic  8.59 us (4%)
  matrix products  7.94 us (4%)
    reduce_scatter x1, waiting for transfers between devices, per_device(): lax.psum_scatter(paired, ('zh', 'zl'), scatter_dimension=0, tiled=True)[0]  68.1 us
    all_gather x1, blocking collectives, gather_block(): high = lax.all_gather(rows_here, 'zh', axis=0, tiled=True)  27.8 us
    all_gather x1, waiting for transfers between devices, gather_block(): mine = lax.all_gather(high, 'zl', axis=0, tiled=True)  11.3 us
    all_to_all x1, starting transfers between devices, per_device(): lax.all_to_all(jnp.broadcast_to(stats[None], (owners, *stats.shape)), 'ce...  8.46 us
    all_to_all x1, waiting for transfers between devices, per_device(): lax.all_to_all(outgoing, 'cent', split_axis=0, concat_axis=0, tiled=True)  7.69 us
    all_to_all x1, starting transfers between devices, per_device(): lax.all_to_all(slot_routes, 'cent', split_axis=0, concat_axis=0, tiled=True)  7.42 us
    all_to_all x1, starting transfers between devices, per_device(): lax.all_to_all(outgoing, 'cent', split_axis=0, concat_axis=0, tiled=True)  5.58 us
    all_to_all x1, waiting for transfers between devices, per_device(): lax.all_to_all(jnp.broadcast_to(stats[None], (owners, *stats.shape)), 'ce...  5.55 us
  transfers between devices with their start and end apart: 7, of which 6 were waited for; matrix products, arithmetic and copies ran while one was open for 6% of the time, Pallas kernels for 0%

profile of v9, /device:TPU:6, one launch (start us, length us, event | category | flops | bytes accessed | tf_op | source)
XLA Modules:
  0.0 194.1 jit_solution(12782710908877234514)
XLA Ops:
  6.5 27.8 %all-gather = bf16[1,128,1024]{2,1,0:T(8,128)(2,1)} all-gather(bf16[1,32,1024]{2,1,0:T(8,128)(2,1)} %param.7), channel_id=2, replica_groups=mesh['zh'=4,'zl'=4,'core'=2,'cent'=16] {'zh'}, dimensions={1}, use_global_device_ids=true | all-gather | bytes 327680 | tf_op jit(solution)/shard_map/all_gather | solution.py:21
  34.4 0.8 iota_compare_fusion.1
  36.0 0.8 fusion.21
  39.2 7.4 %all-to-all-start.1 = ((s32[16,2,3]{2,1,0:T(2,128)}), s32[16,2,3]{2,1,0:T(2,128)S(1)}, u32[]{:S(2)}, u32[]{:S(2)}) async-start(s32[16,2,3]{2,1,0:T(2,128)} %bitcast.7), calls=%async_computation.1 | async-start | bytes 32768 | tf_op jit(solution)/shard_map/all_to_all | solution.py:61
  47.6 2.4 %reshape.133 = bf16[16,64,1024]{2,1,0:T(8,128)(2,1)} reshape(bf16[32,32768]{1,0:T(8,128)(2,1)S(1)} %convolution_convert_fusion) | data formatting | bytes 4194304 | tf_op jit(solution)/shard_map/reshape | solution.py:54
  50.0 2.3 %all-to-all-done.1 = s32[16,2,3]{2,1,0:T(2,128)S(1)} async-done(((s32[16,2,3]{2,1,0:T(2,128)}), s32[16,2,3]{2,1,0:T(2,128)S(1)}, u32[]{:S(2)}, u32[]{:S(2)}) %all-to-all-start.1) | async-done | bytes 416 | tf_op jit(solution)/shard_map/all_to_all | solution.py:61
  52.3 5.6 %all-to-all-start = ((bf16[16,64,1024]{2,1,0:T(8,128)(2,1)}), bf16[16,64,1024]{2,1,0:T(8,128)(2,1)S(1)}, u32[]{:S(2)}, u32[]{:S(2)}) async-start(bf16[16,64,1024]{2,1,0:T(8,128)(2,1)} %reshape.133), calls=%async_computation | async-start | bytes 4194304 | tf_op jit(solution)/shard_map/all_to_all | solution.py:60
  57.9 11.3 %all-gather.4.cloned.1.call-done = bf16[1,512,1024]{2,1,0:T(8,128)(2,1)} async-done(((bf16[1,128,1024]{2,1,0:T(8,128)(2,1)}), bf16[1,512,1024]{2,1,0:T(8,128)(2,1)}) %all-gather.4.cloned.1.call-update) | async-done | bytes 1048592 | tf_op jit(solution)/shard_map/all_gather | solution.py:22
  69.2 1.9 collective-permute-start
  72.0 7.7 %all-to-all-done = bf16[16,64,1024]{2,1,0:T(8,128)(2,1)S(1)} async-done(((bf16[16,64,1024]{2,1,0:T(8,128)(2,1)}), bf16[16,64,1024]{2,1,0:T(8,128)(2,1)S(1)}, u32[]{:S(2)}, u32[]{:S(2)}) %all-to-all-start) | async-done | bytes 2097184 | tf_op jit(solution)/shard_map/all_to_all | solution.py:60
  79.7 3.9 %multiply_reduce_fusion = (f32[1024]{0:T(1024)S(1)}, f32[1024,1024]{0,1:T(8,128)S(1)}) fusion(bf16[1024,1024]{1,0:T(8,128)(2,1)S(1)} %bitcast.61, bf16[512,1024]{1,0:T(8,128)(2,1)} %collective-permute-done, bf16[512,1024]{1,0:T(8,128)(2,1)} %bitcast.74), kind=kOutput, calls=%fused_computation.5 | convolution fusion | flops 2153774080 | bytes 8392704 | tf_op jit(solution)/shard_map/dot_general | solution.py:64
  83.6 1.9 copy-done
  87.0 8.5 %all-to-all-start.2 = ((f32[16,2,1024]{2,1,0:T(2,128)}), f32[16,2,1024]{2,1,0:T(2,128)S(1)}, u32[]{:S(2)}, u32[]{:S(2)}) async-start(f32[16,2,1024]{2,1,0:T(2,128)} %broadcast_in_dim.76), calls=%async_computation.2 | async-start | bytes 262144 | tf_op jit(solution)/shard_map/all_to_all | solution.py:75
  95.7 5.6 %all-to-all-done.2 = f32[16,2,1024]{2,1,0:T(2,128)S(1)} async-done(((f32[16,2,1024]{2,1,0:T(2,128)}), f32[16,2,1024]{2,1,0:T(2,128)S(1)}, u32[]{:S(2)}, u32[]{:S(2)}) %all-to-all-start.2) | async-done | bytes 131104 | tf_op jit(solution)/shard_map/all_to_all | solution.py:75
  102.1 1.5 gather_fusion
  104.0 2.8 %exponential_convert_fusion = bf16[1024,1024]{0,1:T(8,128)(2,1)S(1)} fusion(f32[1024,1024]{0,1:T(8,128)} %copy-done, f32[1024]{0:T(1024)S(1)} %select_n.59), kind=kLoop, calls=%fused_computation.3 | loop fusion | flops 3145728 | bytes 6295552 | tf_op jit(solution)/shard_map/convert_element_type | solution.py:89
  106.9 1.5 fusion.4
  108.4 1.9 collective-permute-start.1
  110.3 1.5 fusion.5
  111.9 3.0 %collective-permute-done.1 = f32[512,1152]{1,0:T(8,128)S(1)} collective-permute-done((f32[512,1152]{1,0:T(8,128)S(1)}, f32[512,1152]{1,0:T(8,128)S(1)}, u32[]{:S(2)}, u32[]{:S(2)}) %collective-permute-start.1) | collective-permute-done | bytes 2359328 | tf_op jit(solution)/shard_map/ppermute | solution.py:103
  115.1 1.6 copy.148
  116.7 68.1 %reduce-scatter.2.cloned.1.call-done = f32[1,32,1152]{2,1,0:T(8,128)} async-done(((f32[16,32,1152]{2,1,0:T(8,128)}), f32[1,32,1152]{2,1,0:T(8,128)}) %reduce-scatter.2.cloned.1.call-update) | async-done | bytes 147472 | tf_op jit(solution)/shard_map/reduce_scatter | solution.py:107
  184.8 0.8 fusion.17
  185.6 1.6 fusion.11
  (59 shorter events, 8.3 us)
Async XLA Ops:
  6.5 62.7 %all-gather.4.cloned.1.call-start = ((), (), s32[]{:S(2)}) async-start(), calls=%async_computation.5 | async-start | bytes 1310720 | tf_op jit(solution)/shard_map/all_gather | solution.py:22
  34.4 3.9 %copy-start.3 = (s32[8]{0:T(128)S(1)}, s32[8]{0:T(128)}, u32[]{:S(2)}) copy-start(s32[8]{0:T(128)} %param.6) | copy-start | bytes 100
  34.4 12.3 %copy-start.1 = (bf16[256,1024]{1,0:T(8,128)(2,1)S(1)}, bf16[256,1024]{1,0:T(8,128)(2,1)}, u32[]{:S(2)}) copy-start(bf16[256,1024]{1,0:T(8,128)(2,1)} %param.4) | copy-start | bytes 1572868
  39.2 13.0 %all-to-all-start.1 = ((s32[16,2,3]{2,1,0:T(2,128)}), s32[16,2,3]{2,1,0:T(2,128)S(1)}, u32[]{:S(2)}, u32[]{:S(2)}) async-start(s32[16,2,3]{2,1,0:T(2,128)} %bitcast.7), calls=%async_computation.1 | async-start | bytes 32768 | tf_op jit(solution)/shard_map/all_to_all | solution.py:61
  52.3 27.4 %all-to-all-start = ((bf16[16,64,1024]{2,1,0:T(8,128)(2,1)}), bf16[16,64,1024]{2,1,0:T(8,128)(2,1)S(1)}, u32[]{:S(2)}, u32[]{:S(2)}) async-start(bf16[16,64,1024]{2,1,0:T(8,128)(2,1)} %reshape.133), calls=%async_computation | async-start | bytes 4194304 | tf_op jit(solution)/shard_map/all_to_all | solution.py:60
  69.2 10.5 %collective-permute-start = (bf16[512,1024]{1,0:T(8,128)(2,1)}, bf16[512,1024]{1,0:T(8,128)(2,1)}, u32[]{:S(2)}, u32[]{:S(2)}) collective-permute-start(bf16[512,1024]{1,0:T(8,128)(2,1)} %bitcast.73), channel_id=1, source_target_pairs={{0,16},{16,0},{1,17},{17,1},{2,18},{18,2},{3,19},{19,3},{4,20},{20... | collective-permute-start | bytes 3145736 | tf_op jit(solution)/shard_map/ppermute | solution.py:23
  83.6 1.9 copy-start
  87.0 14.3 %all-to-all-start.2 = ((f32[16,2,1024]{2,1,0:T(2,128)}), f32[16,2,1024]{2,1,0:T(2,128)S(1)}, u32[]{:S(2)}, u32[]{:S(2)}) async-start(f32[16,2,1024]{2,1,0:T(2,128)} %broadcast_in_dim.76), calls=%async_computation.2 | async-start | bytes 262144 | tf_op jit(solution)/shard_map/all_to_all | solution.py:75
  95.4 89.4 %reduce-scatter.2.cloned.1.call-start = ((), (), s32[]{:S(2)}) async-start(), calls=%async_computation.4 | async-start | bytes 2506752 | tf_op jit(solution)/shard_map/reduce_scatter | solution.py:107
  108.4 6.4 %collective-permute-start.1 = (f32[512,1152]{1,0:T(8,128)S(1)}, f32[512,1152]{1,0:T(8,128)S(1)}, u32[]{:S(2)}, u32[]{:S(2)}) collective-permute-start(f32[512,1152]{1,0:T(8,128)S(1)} %fusion.4), channel_id=1, source_target_pairs={{0,16},{16,0},{1,17},{17,1},{2,18},{18,2},{3,19},{19,3},{4,20},{20... | collective-permute-start | bytes 7077896 | tf_op jit(solution)/shard_map/ppermute | solution.py:103
  116.7 68.9 %copy-start.2 = (bf16[1,32,1024]{2,1,0:T(8,128)(2,1)S(1)}, bf16[1,32,1024]{2,1,0:T(8,128)(2,1)}, u32[]{:S(2)}) copy-start(bf16[1,32,1024]{2,1,0:T(8,128)(2,1)} %param.7) | copy-start | bytes 196612
Sparse Core Ops, SparseCore 0:
  34.5 34.6 all-gather.3
  116.8 67.9 reduce-scatter.1
